TPU v7x, 256 devices: a whole 4x4x8 slice. The times are simulated.
256 devices in a mesh: gx: 64 (over z, y, core), gy: 4 (over x).
Axes of the slice: x: 4, y: 4, z: 8, core: 2. Of those that a mesh axis runs over, the one named last changes fastest.
Arguments:
- embeds: bfloat16 [256, 2048, 768], P('gx', 'gy'), may hold values from -6 to 6
- fetch_list: int32 [2, 64, 64], replicated, may hold values from 0 to 16383, as said below
- partners: int32 [2, 64, 64, 2], replicated, may hold values from 0 to 255, as said below
- counts: int32 [256], replicated, may hold values from 512 to 2048
Outputs:
- nearest: float32 [256, 2048], P('gx', 'gy')
Inputs may be any that keep to these rules, and one draw needn't show every extreme that they name: fetch_list[w, h, g] // 64 is a block stored by index g of gx, that is g * 4 <= fetch_list[w, h, g] // 64 < (g + 1) * 4. partners[w, h, g, :] are 2 different blocks stored by index h of gx, none equal to fetch_list[w, h, g] // 64.
All inputs are finite; a program needn't handle non-finite values.
Results may differ from a plain program's by a relative error of at most 0.0003.
Values may be sent and summed in bfloat16 or wider, within the bound.
No kernel may reach another device: no remote copies, remote signals or barrier semaphores. Data moves between devices by JAX's collectives and lax.ppermute only.
A program may use at most 192 MiB of HBM per device.

v0:
```python
import jax
import jax.numpy as jnp
from jax import lax
from jax.sharding import PartitionSpec as P


SLICE = 8


EPS = 1e-06


def normalize(source):
    values = source.astype(jnp.float32)
    return (values * lax.rsqrt(jnp.sum(values * values, axis=-1, keepdims=True) + EPS)).astype(
        jnp.bfloat16
    )


def lent_scores(lent, row_valid, listed, columns, col_limit):
    slots, lent_rows, width = lent.shape
    owned, quarter, _ = columns.shape
    flat_rows = lent.reshape(slots * lent_rows, width)
    scores = jnp.einsum("rd,kcd->rkc", flat_rows, columns, preferred_element_type=jnp.float32)
    scores = scores.reshape(slots, lent_rows, owned, quarter)
    col_valid = jnp.arange(quarter, dtype=jnp.int32)[None, :] < col_limit[:, None]
    keep = row_valid[:, :, None, None] & listed[:, None, :, None] & col_valid[None, None, :, :]
    scores = jnp.where(keep, scores, jnp.float32(-1.0))
    return jnp.max(scores, axis=(2, 3)), jnp.max(scores, axis=(0, 1))


def device_body(embeds, fetch_list, partners, counts):
    owned, quarter, width = embeds.shape
    slice_rows = SLICE
    pieces = quarter // slice_rows
    my_group = lax.axis_index("gx")
    my_lane = lax.axis_index("gy")
    n_gy = lax.axis_size("gy")
    first = my_group * owned
    waves = fetch_list.shape[0]
    pair_p = [(lane, lane ^ 1) for lane in range(n_gy)]
    pair_r = [(lane, n_gy - 1 - lane) for lane in range(n_gy)]
    lane_p = jnp.bitwise_xor(my_lane, 1)
    lane_r = n_gy - 1 - my_lane
    own_unit = normalize(embeds)
    other_unit = lax.ppermute(own_unit, "gy", pair_p)
    own_pieces = own_unit.reshape(owned, pieces, slice_rows, width)
    own_counts = lax.dynamic_slice_in_dim(counts, first, owned)
    positions = jnp.arange(quarter, dtype=jnp.int32)
    col_sources = []
    for lane, unit in ((my_lane, own_unit), (lane_p, other_unit)):
        col_limit = (own_counts - lane * quarter).astype(jnp.int32)
        col_sources.append((unit, col_limit))
    slice_offsets = jnp.arange(slice_rows, dtype=jnp.int32)
    local_ids = jnp.arange(owned, dtype=jnp.int32)
    piece_ids = jnp.arange(pieces, dtype=jnp.int32)
    col_part = [jnp.full((owned, quarter), -1.0, jnp.float32) for _ in col_sources]
    sent_blocks = []
    sent_pieces = []
    jobs = []
    for wave_index in range(waves):
        tiles = lax.dynamic_index_in_dim(fetch_list[wave_index], my_group, 1, False)
        outgoing_sent_block = tiles // pieces - first
        outgoing_sent_piece = tiles % pieces
        sent_blocks.append(outgoing_sent_block)
        sent_pieces.append(outgoing_sent_piece)
        outbound = own_pieces[outgoing_sent_block, outgoing_sent_piece]
        arrived = lax.all_to_all(outbound, "gx", split_axis=0, concat_axis=0, tiled=True)
        arrived_other = lax.ppermute(arrived, "gy", pair_r)
        incoming = lax.dynamic_index_in_dim(fetch_list[wave_index], my_group, 0, False)
        arrived_counts = counts[incoming // pieces]
        chosen = lax.dynamic_index_in_dim(partners[wave_index], my_group, 0, False) - first
        listed = jnp.any(chosen[:, :, None] == local_ids[None, None, :], axis=1)
        piece_rows = (incoming % pieces)[:, None] * slice_rows + slice_offsets[None, :]
        for part, (lane, rows_in) in enumerate(((my_lane, arrived), (lane_r, arrived_other))):
            row_valid = (lane * quarter + piece_rows) < arrived_counts[:, None]
            jobs.append((wave_index, part, rows_in, row_valid, listed))
    row_best = {}
    token = None
    order = sorted(
        ((source, job) for source in range(len(col_sources)) for job in range(len(jobs))),
        key=lambda item: (jobs[item[1]][0] == waves - 1 and jobs[item[1]][1] == 1, item[0], item[1]),
    )
    for source, job in order:
        unit, col_limit = col_sources[source]
        wave_index, part, rows_in, row_valid, listed = jobs[job]
        if token is not None:
            token, rows_in, unit = lax.optimization_barrier((token, rows_in, unit))
        rows_max, col_best = lent_scores(rows_in, row_valid, listed, unit, col_limit)
        token = (rows_max, col_best)
        key = (wave_index, part)
        row_best[key] = rows_max if key not in row_best else jnp.maximum(row_best[key], rows_max)
        col_part[source] = jnp.maximum(col_part[source], col_best)
    row_mine_parts = [row_best[(wave_index, 0)] for wave_index in range(waves)]
    row_other_parts = [row_best[(wave_index, 1)] for wave_index in range(waves)]
    col_back = lax.ppermute(col_part[1], "gy", pair_p)
    col_total = jnp.maximum(col_part[0], col_back)
    row_other = jnp.stack(row_other_parts, axis=0)
    row_back = lax.ppermute(row_other, "gy", pair_r)
    row_mine = jnp.maximum(jnp.stack(row_mine_parts, axis=0), row_back)
    returned = lax.all_to_all(row_mine, "gx", split_axis=1, concat_axis=1, tiled=True)
    row_total = jnp.full((owned, pieces, slice_rows), -1.0, jnp.float32)
    for wave_index in range(waves):
        match = (sent_blocks[wave_index][:, None, None] == local_ids[None, :, None]) & (
            sent_pieces[wave_index][:, None, None] == piece_ids[None, None, :]
        )
        placed = jnp.max(
            jnp.where(
                match[:, :, :, None], returned[wave_index][:, None, None, :], jnp.float32(-1.0)
            ),
            axis=0,
        )
        row_total = jnp.maximum(row_total, placed)
    nearest = jnp.maximum(row_total.reshape(owned, quarter), col_total)
    mine_valid = (my_lane * quarter + positions)[None, :] < own_counts[:, None]
    return jnp.where(mine_valid, nearest, jnp.float32(-1.0))


def solution(mesh):
    in_specs = (P("gx", "gy", None), P(), P(), P())
    out_specs = P("gx", "gy")
    return jax.shard_map(
        device_body, mesh=mesh, in_specs=in_specs, out_specs=out_specs, check_vma=False
    )
```

profile of v0, /device:TPU:1, one launch (start us, length us, event | category | flops | bytes accessed | tf_op | source)
XLA Modules:
  0.0 145.7 jit_solution(7436641130911203204)
XLA Ops:
  0.9 2.6 %fusion = f32[4,512]{1,0:T(4,128)S(1)} fusion(bf16[4,512,768]{2,1,0:T(8,128)(2,1)} %param.4), kind=kLoop, calls=%fused_computation.6 | loop fusion | flops 4716544 | bytes 3153920 | tf_op jit(solution)/shard_map/reduce_sum | solution.py:15
  3.6 2.3 %fusion.71 = bf16[4,64,8,768]{3,2,1,0:T(8,128)(2,1)} fusion(f32[4,512]{1,0:T(4,128)S(1)} %add_rsqrt_fusion, bf16[4,512,768]{2,1,0:T(8,128)(2,1)S(1)} %copy-done.1), kind=kLoop, calls=%fused_computation.172 | loop fusion | flops 4718592 | bytes 6299648 | tf_op jit(solution)/shard_map/reshape | solution.py:47
  6.1 3.5 %gather_fusion.1 = bf16[64,8,768]{2,1,0:T(8,128)(2,1)} fusion(bf16[4,64,8,768]{3,2,1,0:T(8,128)(2,1)} %fusion.71, s32[64]{0:T(128)S(1)} %fusion.65), kind=kCustom, calls=%fused_computation.1 | custom fusion | bytes 1573376 | tf_op jit(solution)/shard_map/gather | solution.py:67
  9.6 13.3 %all-to-all-start = ((bf16[64,8,768]{2,1,0:T(8,128)(2,1)}), bf16[64,8,768]{2,1,0:T(8,128)(2,1)}, u32[]{:S(2)}, u32[]{:S(2)}) async-start(bf16[64,8,768]{2,1,0:T(8,128)(2,1)} %gather_fusion.1), calls=%async_computation | async-start | bytes 1572864 | tf_op jit(solution)/shard_map/all_to_all | solution.py:68
  22.9 2.2 %fusion.1 = bf16[4,512,768]{2,1,0:T(8,128)(2,1)} fusion(bf16[4,512,768]{2,1,0:T(8,128)(2,1)S(1)} %copy-done.1, f32[4,512]{1,0:T(4,128)S(1)} %add_rsqrt_fusion), kind=kLoop, calls=%fused_computation.7 | loop fusion | flops 4718592 | bytes 6299648 | tf_op jit(solution)/shard_map/convert_element_type | solution.py:15
  28.7 3.5 %gather_fusion.3 = bf16[64,8,768]{2,1,0:T(8,128)(2,1)} fusion(bf16[4,64,8,768]{3,2,1,0:T(8,128)(2,1)} %fusion.71, s32[64]{0:T(128)S(1)} %fusion.64), kind=kCustom, calls=%fused_computation.3 | custom fusion | bytes 1573376 | tf_op jit(solution)/shard_map/gather | solution.py:67
  32.6 13.2 %all-to-all-done = bf16[64,8,768]{2,1,0:T(8,128)(2,1)} async-done(((bf16[64,8,768]{2,1,0:T(8,128)(2,1)}), bf16[64,8,768]{2,1,0:T(8,128)(2,1)}, u32[]{:S(2)}, u32[]{:S(2)}) %all-to-all-start) | async-done | bytes 786464 | tf_op jit(solution)/shard_map/all_to_all | solution.py:68
  45.8 5.9 %all-to-all-start.1 = ((bf16[64,8,768]{2,1,0:T(8,128)(2,1)}), bf16[64,8,768]{2,1,0:T(8,128)(2,1)S(1)}, u32[]{:S(2)}, u32[]{:S(2)}) async-start(bf16[64,8,768]{2,1,0:T(8,128)(2,1)} %gather_fusion.3), calls=%async_computation.1 | async-start | bytes 1572864 | tf_op jit(solution)/shard_map/all_to_all | solution.py:68
  52.3 2.6 %collective-permute-start = (bf16[64,8,768]{2,1,0:T(8,128)(2,1)}, bf16[64,8,768]{2,1,0:T(8,128)(2,1)S(1)}, u32[]{:S(2)}, u32[]{:S(2)}) collective-permute-start(bf16[64,8,768]{2,1,0:T(8,128)(2,1)} %all-to-all-done), channel_id=1, source_target_pairs={{0,3},{1,2},{2,1},{3,0},{4,7},{5,6},{6,5},{7,4},{8,11},{9,10},{10,... | collective-permute-start | bytes 2359304 | tf_op jit(solution)/shard_map/ppermute | solution.py:69
  55.4 19.4 %all-to-all-done.1 = bf16[64,8,768]{2,1,0:T(8,128)(2,1)S(1)} async-done(((bf16[64,8,768]{2,1,0:T(8,128)(2,1)}), bf16[64,8,768]{2,1,0:T(8,128)(2,1)S(1)}, u32[]{:S(2)}, u32[]{:S(2)}) %all-to-all-start.1) | async-done | bytes 786464 | tf_op jit(solution)/shard_map/all_to_all | solution.py:68
  74.7 2.5 %collective-permute-start.2 = (bf16[64,8,768]{2,1,0:T(8,128)(2,1)S(1)}, bf16[64,8,768]{2,1,0:T(8,128)(2,1)S(1)}, u32[]{:S(2)}, u32[]{:S(2)}) collective-permute-start(bf16[64,8,768]{2,1,0:T(8,128)(2,1)S(1)} %all-to-all-done.1), channel_id=1, source_target_pairs={{0,3},{1,2},{2,1},{3,0},{4,7},{5,6},{6,5},{7,4},{8,11},{9,10},{10,... | collective-permute-start | bytes 2359304 | tf_op jit(solution)/shard_map/ppermute | solution.py:69
  77.2 4.2 %fusion.2 = (f32[4,512]{1,0:T(4,128)S(1)}, f32[64,8]{1,0:T(8,128)S(1)}) fusion(pred[4,512]{1,0:T(4,128)(4,1)S(1)} %iota_compare_fusion.5, pred[64,8,4]{1,2,0:T(4,128)(4,1)S(1)} %get-tuple-element.60, bf16[4,512,768]{2,1,0:T(8,128)(2,1)} %fusion.1, bf16[64,8,768]{2,1,0:T(8,128)(2,1)} %all-to-all-done), kind=kOutput, calls=%fused_computation.16 | convolution fusion | flops 1614804480 | bytes 3946496 | tf_op jit(solution)/shard_map/rd,kcd->rkc/dot_general | solution.py:24
  81.4 4.5 %fusion.8 = (f32[4,512]{1,0:T(4,128)S(1)}, f32[64,8]{1,0:T(8,128)S(1)}) fusion(pred[64,8,4]{1,2,0:T(4,128)(4,1)S(1)} %get-tuple-element.59, pred[4,512]{1,0:T(4,128)(4,1)S(1)} %iota_compare_fusion.5, bf16[4,512,768]{2,1,0:T(8,128)(2,1)} %fusion.1, bf16[64,8,768]{2,1,0:T(8,128)(2,1)S(1)} %collective-permute-done), kind=kOutput, calls=%fused_computation.22 | convolution fusion | flops 1614804480 | bytes 3946496 | tf_op jit(solution)/shard_map/rd,kcd->rkc/dot_general | solution.py:24
  85.9 4.4 %fusion.6 = (f32[4,512]{1,0:T(4,128)S(1)}, f32[64,8]{1,0:T(8,128)S(1)}) fusion(pred[64,8,4]{1,2,0:T(4,128)(4,1)S(1)} %get-tuple-element.58, pred[4,512]{1,0:T(4,128)(4,1)S(1)} %iota_compare_fusion.5, bf16[4,512,768]{2,1,0:T(8,128)(2,1)} %fusion.1, bf16[64,8,768]{2,1,0:T(8,128)(2,1)S(1)} %all-to-all-done.1), kind=kOutput, calls=%fused_computation.20 | convolution fusion | flops 1614804480 | bytes 3946496 | tf_op jit(solution)/shard_map/rd,kcd->rkc/dot_general | solution.py:24
  90.3 4.3 %collective-permute-done.1 = bf16[4,512,768]{2,1,0:T(8,128)(2,1)} collective-permute-done((bf16[4,512,768]{2,1,0:T(8,128)(2,1)}, bf16[4,512,768]{2,1,0:T(8,128)(2,1)}, u32[]{:S(2)}, u32[]{:S(2)}) %collective-permute-start.1) | collective-permute-done | bytes 3145760 | tf_op jit(solution)/shard_map/ppermute | solution.py:46
  94.6 4.2 %fusion.4 = (f32[4,512]{1,0:T(4,128)S(1)}, f32[64,8]{1,0:T(8,128)S(1)}) fusion(pred[4,512]{1,0:T(4,128)(4,1)S(1)} %iota_compare_fusion.4, pred[64,8,4]{1,2,0:T(4,128)(4,1)S(1)} %get-tuple-element.60, bf16[4,512,768]{2,1,0:T(8,128)(2,1)} %collective-permute-done.1, bf16[64,8,768]{2,1,0:T(8,128)(2,1)} %all-to-all-done), kind=kOutput, calls=%fused_computation.18 | convolution fusion | flops 1614804480 | bytes 3946496 | tf_op jit(solution)/shard_map/rd,kcd->rkc/dot_general | solution.py:24
  98.8 4.5 %fusion.12 = (f32[4,512]{1,0:T(4,128)S(1)}, f32[64,8]{1,0:T(8,128)S(1)}) fusion(pred[64,8,4]{1,2,0:T(4,128)(4,1)S(1)} %get-tuple-element.59, pred[4,512]{1,0:T(4,128)(4,1)S(1)} %iota_compare_fusion.4, bf16[4,512,768]{2,1,0:T(8,128)(2,1)} %collective-permute-done.1, bf16[64,8,768]{2,1,0:T(8,128)(2,1)S(1)} %collective-permute-done), kind=kOutput, calls=%fused_computation.26 | convolution fusion | flops 1614804480 | bytes 3946496 | tf_op jit(solution)/shard_map/rd,kcd->rkc/dot_general | solution.py:24
  103.2 4.5 %fusion.10 = (f32[4,512]{1,0:T(4,128)S(1)}, f32[64,8]{1,0:T(8,128)S(1)}) fusion(pred[64,8,4]{1,2,0:T(4,128)(4,1)S(1)} %get-tuple-element.58, pred[4,512]{1,0:T(4,128)(4,1)S(1)} %iota_compare_fusion.4, bf16[4,512,768]{2,1,0:T(8,128)(2,1)} %collective-permute-done.1, bf16[64,8,768]{2,1,0:T(8,128)(2,1)S(1)} %all-to-all-done.1), kind=kOutput, calls=%fused_computation.24 | convolution fusion | flops 1614804480 | bytes 3946496 | tf_op jit(solution)/shard_map/rd,kcd->rkc/dot_general | solution.py:24
  107.7 4.5 %fusion.14 = (f32[4,512]{1,0:T(4,128)S(1)}, f32[64,8]{1,0:T(8,128)S(1)}) fusion(pred[64,8,4]{1,2,0:T(4,128)(4,1)S(1)} %get-tuple-element.57, pred[4,512]{1,0:T(4,128)(4,1)S(1)} %iota_compare_fusion.5, bf16[4,512,768]{2,1,0:T(8,128)(2,1)} %fusion.1, bf16[64,8,768]{2,1,0:T(8,128)(2,1)S(1)} %collective-permute-done.2), kind=kOutput, calls=%fused_computation.28 | convolution fusion | flops 1614804480 | bytes 3946496 | tf_op jit(solution)/shard_map/rd,kcd->rkc/dot_general | solution.py:24
  112.2 4.4 %fusion.16 = (f32[4,512]{1,0:T(4,128)S(1)}, f32[64,8]{1,0:T(8,128)S(1)}) fusion(pred[64,8,4]{1,2,0:T(4,128)(4,1)S(1)} %get-tuple-element.57, pred[4,512]{1,0:T(4,128)(4,1)S(1)} %iota_compare_fusion.4, bf16[4,512,768]{2,1,0:T(8,128)(2,1)} %collective-permute-done.1, bf16[64,8,768]{2,1,0:T(8,128)(2,1)S(1)} %collective-permute-done.2), kind=kOutput, calls=%fused_computation.30 | convolution fusion | flops 1614804480 | bytes 3946496 | tf_op jit(solution)/shard_map/rd,kcd->rkc/dot_general | solution.py:24
  116.6 2.6 %collective-permute-start.3 = (f32[2,64,8]{2,1,0:T(8,128)S(1)}, f32[2,64,8]{2,1,0:T(8,128)S(1)}, u32[]{:S(2)}, u32[]{:S(2)}) collective-permute-start(f32[2,64,8]{2,1,0:T(8,128)S(1)} %pad_maximum_fusion), channel_id=1, source_target_pairs={{0,3},{1,2},{2,1},{3,0},{4,7},{5,6},{6,5},{7,4},{8,11},{9,10},{10,... | collective-permute-start | bytes 12296 | tf_op jit(solution)/shard_map/ppermute | solution.py:99
  119.2 1.8 %collective-permute-done.3 = f32[2,64,8]{2,1,0:T(8,128)S(1)} collective-permute-done((f32[2,64,8]{2,1,0:T(8,128)S(1)}, f32[2,64,8]{2,1,0:T(8,128)S(1)}, u32[]{:S(2)}, u32[]{:S(2)}) %collective-permute-start.3) | collective-permute-done | bytes 4128 | tf_op jit(solution)/shard_map/ppermute | solution.py:99
  121.7 12.4 %all-to-all-start.2 = ((f32[2,64,8]{2,0,1:T(2,128)}), f32[2,64,8]{2,0,1:T(2,128)S(1)}, u32[]{:S(2)}, u32[]{:S(2)}) async-start(f32[2,64,8]{2,0,1:T(2,128)} %copy.31), calls=%async_computation.2 | async-start | bytes 131072 | tf_op jit(solution)/shard_map/all_to_all | solution.py:101
  134.3 10.0 %all-to-all-done.2 = f32[2,64,8]{2,0,1:T(2,128)S(1)} async-done(((f32[2,64,8]{2,0,1:T(2,128)}), f32[2,64,8]{2,0,1:T(2,128)S(1)}, u32[]{:S(2)}, u32[]{:S(2)}) %all-to-all-start.2) | async-done | bytes 4128 | tf_op jit(solution)/shard_map/all_to_all | solution.py:101
  (65 shorter events, 8.2 us)
Async XLA Ops:
  0.0 3.6 %copy-start.1 = (bf16[4,512,768]{2,1,0:T(8,128)(2,1)S(1)}, bf16[4,512,768]{2,1,0:T(8,128)(2,1)}, u32[]{:S(2)}) copy-start(bf16[4,512,768]{2,1,0:T(8,128)(2,1)} %param.4) | copy-start | bytes 9437188
  9.6 36.3 %all-to-all-start = ((bf16[64,8,768]{2,1,0:T(8,128)(2,1)}), bf16[64,8,768]{2,1,0:T(8,128)(2,1)}, u32[]{:S(2)}, u32[]{:S(2)}) async-start(bf16[64,8,768]{2,1,0:T(8,128)(2,1)} %gather_fusion.1), calls=%async_computation | async-start | bytes 1572864 | tf_op jit(solution)/shard_map/all_to_all | solution.py:68
  22.9 3.8 %copy-start = (s32[256]{0:T(256)S(1)}, s32[256]{0:T(256)}, u32[]{:S(2)}) copy-start(s32[256]{0:T(256)} %param.7) | copy-start | bytes 3076
  22.9 5.5 %copy-start.2 = (s32[2,64,64,2]{2,3,1,0:T(2,128)S(1)}, s32[2,64,64,2]{2,3,1,0:T(2,128)}, u32[]{:S(2)}) copy-start(s32[2,64,64,2]{2,3,1,0:T(2,128)} %param.6) | copy-start | bytes 196612
  25.2 69.5 %collective-permute-start.1 = (bf16[4,512,768]{2,1,0:T(8,128)(2,1)}, bf16[4,512,768]{2,1,0:T(8,128)(2,1)}, u32[]{:S(2)}, u32[]{:S(2)}) collective-permute-start(bf16[4,512,768]{2,1,0:T(8,128)(2,1)} %fusion.1), channel_id=1, source_target_pairs={{0,1},{1,0},{2,3},{3,2},{4,5},{5,4},{6,7},{7,6},{8,9},{9,8},{10,11... | collective-permute-start | bytes 9437192 | tf_op jit(solution)/shard_map/ppermute | solution.py:46
  45.8 28.9 %all-to-all-start.1 = ((bf16[64,8,768]{2,1,0:T(8,128)(2,1)}), bf16[64,8,768]{2,1,0:T(8,128)(2,1)S(1)}, u32[]{:S(2)}, u32[]{:S(2)}) async-start(bf16[64,8,768]{2,1,0:T(8,128)(2,1)} %gather_fusion.3), calls=%async_computation.1 | async-start | bytes 1572864 | tf_op jit(solution)/shard_map/all_to_all | solution.py:68
  52.3 29.1 %collective-permute-start = (bf16[64,8,768]{2,1,0:T(8,128)(2,1)}, bf16[64,8,768]{2,1,0:T(8,128)(2,1)S(1)}, u32[]{:S(2)}, u32[]{:S(2)}) collective-permute-start(bf16[64,8,768]{2,1,0:T(8,128)(2,1)} %all-to-all-done), channel_id=1, source_target_pairs={{0,3},{1,2},{2,1},{3,0},{4,7},{5,6},{6,5},{7,4},{8,11},{9,10},{10,... | collective-permute-start | bytes 2359304 | tf_op jit(solution)/shard_map/ppermute | solution.py:69
  74.7 33.0 %collective-permute-start.2 = (bf16[64,8,768]{2,1,0:T(8,128)(2,1)S(1)}, bf16[64,8,768]{2,1,0:T(8,128)(2,1)S(1)}, u32[]{:S(2)}, u32[]{:S(2)}) collective-permute-start(bf16[64,8,768]{2,1,0:T(8,128)(2,1)S(1)} %all-to-all-done.1), channel_id=1, source_target_pairs={{0,3},{1,2},{2,1},{3,0},{4,7},{5,6},{6,5},{7,4},{8,11},{9,10},{10,... | collective-permute-start | bytes 2359304 | tf_op jit(solution)/shard_map/ppermute | solution.py:69
  116.6 4.4 %collective-permute-start.3 = (f32[2,64,8]{2,1,0:T(8,128)S(1)}, f32[2,64,8]{2,1,0:T(8,128)S(1)}, u32[]{:S(2)}, u32[]{:S(2)}) collective-permute-start(f32[2,64,8]{2,1,0:T(8,128)S(1)} %pad_maximum_fusion), channel_id=1, source_target_pairs={{0,3},{1,2},{2,1},{3,0},{4,7},{5,6},{6,5},{7,4},{8,11},{9,10},{10,... | collective-permute-start | bytes 12296 | tf_op jit(solution)/shard_map/ppermute | solution.py:99
  121.7 22.5 %all-to-all-start.2 = ((f32[2,64,8]{2,0,1:T(2,128)}), f32[2,64,8]{2,0,1:T(2,128)S(1)}, u32[]{:S(2)}, u32[]{:S(2)}) async-start(f32[2,64,8]{2,0,1:T(2,128)} %copy.31), calls=%async_computation.2 | async-start | bytes 131072 | tf_op jit(solution)/shard_map/all_to_all | solution.py:101
  134.2 10.8 %collective-permute-start.4 = (f32[4,512]{1,0:T(4,128)S(1)}, f32[4,512]{1,0:T(4,128)S(1)}, u32[]{:S(2)}, u32[]{:S(2)}) collective-permute-start(f32[4,512]{1,0:T(4,128)S(1)} %maximum_maximum_fusion.2), channel_id=1, source_target_pairs={{0,1},{1,0},{2,3},{3,2},{4,5},{5,4},{6,7},{7,6},{8,9},{9,8},{10,11... | collective-permute-start | bytes 24584 | tf_op jit(solution)/shard_map/ppermute | solution.py:96
where the time goes:
time: 146 us
  waiting for transfers between devices  48.7 us (33%)
  starting transfers between devices  40.6 us (28%)
  matrix products  35 us (24%)
  local copies, waits for them, and re-layouts  11.5 us (8%)
  other arithmetic  9.6 us (7%)
    dot_general x8, matrix products, lent_scores(): jnp.einsum('rd,kcd->rkc', flat_rows, columns, preferred_element_type=jnp....  35 us
    all_to_all x2, waiting for transfers between devices, device_body(): lax.all_to_all(outbound, 'gx', split_axis=0, concat_axis=0, tiled=True)  32.6 us
    all_to_all x2, starting transfers between devices, device_body(): lax.all_to_all(outbound, 'gx', split_axis=0, concat_axis=0, tiled=True)  19.2 us
    all_to_all x1, starting transfers between devices, device_body(): lax.all_to_all(row_mine, 'gx', split_axis=1, concat_axis=1, tiled=True)  12.4 us
    all_to_all x1, waiting for transfers between devices, device_body(): lax.all_to_all(row_mine, 'gx', split_axis=1, concat_axis=1, tiled=True)  9.97 us
    gather x2, local copies, waits for them, and re-layouts, device_body(): outbound = own_pieces[outgoing_sent_block, outgoing_sent_piece]  7 us
    ppermute x2, starting transfers between devices, device_body(): arrived_other = lax.ppermute(arrived, 'gy', pair_r)  5.04 us
    ppermute x1, waiting for transfers between devices, device_body(): other_unit = lax.ppermute(own_unit, 'gy', pair_p)  4.32 us
  transfers between devices with their start and end apart: 8, of which 5 were waited for; matrix products, arithmetic and copies ran while one was open for 25% of the time, Pallas kernels for 0%

commit v1 on v0

--- a/solution.py
+++ b/solution.py
@@ -1,6 +1,8 @@
 import jax
 import jax.numpy as jnp
 from jax import lax
+from jax.experimental import pallas as pl
+from jax.experimental.pallas import tpu as pltpu
 from jax.sharding import PartitionSpec as P
 
 
@@ -10,11 +12,25 @@
 EPS = 1e-06
 
 
+def _normalize_kernel(source_ref, unit_ref):
+    values = source_ref[0].astype(jnp.float32)
+    scale = lax.rsqrt(jnp.sum(values * values, axis=-1, keepdims=True) + EPS)
+    unit_ref[0] = (values * scale).astype(unit_ref.dtype)
+
+
 def normalize(source):
-    values = source.astype(jnp.float32)
-    return (values * lax.rsqrt(jnp.sum(values * values, axis=-1, keepdims=True) + EPS)).astype(
-        jnp.bfloat16
-    )
+    owned, rows, width = source.shape
+    return pl.pallas_call(
+        _normalize_kernel,
+        out_shape=jax.ShapeDtypeStruct(source.shape, jnp.bfloat16),
+        grid=(owned,),
+        in_specs=[pl.BlockSpec((1, rows, width), lambda k: (k, 0, 0))],
+        out_specs=pl.BlockSpec((1, rows, width), lambda k: (k, 0, 0)),
+        compiler_params=pltpu.CompilerParams(dimension_semantics=("arbitrary",)),
+        cost_estimate=pl.CostEstimate(
+            flops=3 * source.size, transcendentals=owned * rows, bytes_accessed=4 * source.size
+        ),
+    )(source)
 
 
 def lent_scores(lent, row_valid, listed, columns, col_limit):

time: 146 us -> 131 us (0.90)
  starting transfers between devices: 40.6 us -> 33.1 us
  other arithmetic: 9.6 us -> 2.46 us
  matrix products: 35 us -> 29.7 us
  Pallas kernels: 0 us -> 4.66 us
  waiting for transfers between devices: 48.7 us -> 52 us
  local copies, waits for them, and re-layouts: 11.5 us -> 8.64 us
    all_to_all x2, waiting for transfers between devices: 32.6 us -> 38.5 us  [device_body(): lax.all_to_all(outbound, 'gx', split_axis=0, concat_axis=0, tiled=True)]
    dot_general x8, matrix products: 35 us -> 29.7 us  [lent_scores(): jnp.einsum('rd,kcd->rkc', flat_rows, columns, preferred_element_type=jnp....]
    all_to_all x1, starting transfers between devices: 12.4 us -> 7.33 us  [device_body(): lax.all_to_all(row_mine, 'gx', split_axis=1, concat_axis=1, tiled=True)]
    pallas_call x0 -> x1, Pallas kernels: none -> 4.66 us  [normalize(): pl.pallas_call(_normalize_kernel, out_shape=jax.ShapeDtypeStruct(source.s...]
    ppermute x1, waiting for transfers between devices: 4.32 us -> 0.01 us  [device_body(): other_unit = lax.ppermute(own_unit, 'gy', pair_p)]
    reduce_sum x1 -> x0, other arithmetic: 2.62 us -> none  [normalize(): jnp.sum(values * values, axis=-1, keepdims=True) + EPS]
    reshape x1 -> x0, other arithmetic: 2.28 us -> none  [device_body(): own_pieces = own_unit.reshape(owned, pieces, slice_rows, width)]
    convert_element_type x1 -> x0, other arithmetic: 2.24 us -> none  [normalize(): (values * lax.rsqrt(jnp.sum(values * values, axis=-1, keepdims=True) + EP...]
  transfers between devices with their start and end apart: 8 -> 8, of which waited for: 5 -> 4; matrix products, arithmetic and copies ran while one was open for 25% -> 25% of each run, Pallas kernels for 0% -> 0%
where the time goes in v1:
time: 131 us
  waiting for transfers between devices  52 us (40%)
  starting transfers between devices  33.1 us (25%)
  matrix products  29.7 us (23%)
  local copies, waits for them, and re-layouts  8.64 us (7%)
  Pallas kernels  4.66 us (4%)
  other arithmetic  2.46 us (2%)
    all_to_all x2, waiting for transfers between devices, device_body(): lax.all_to_all(outbound, 'gx', split_axis=0, concat_axis=0, tiled=True)  38.5 us
    dot_general x8, matrix products, lent_scores(): jnp.einsum('rd,kcd->rkc', flat_rows, columns, preferred_element_type=jnp....  29.7 us
    all_to_all x2, starting transfers between devices, device_body(): lax.all_to_all(outbound, 'gx', split_axis=0, concat_axis=0, tiled=True)  18.8 us
    all_to_all x1, waiting for transfers between devices, device_body(): lax.all_to_all(row_mine, 'gx', split_axis=1, concat_axis=1, tiled=True)  9.97 us
    all_to_all x1, starting transfers between devices, device_body(): lax.all_to_all(row_mine, 'gx', split_axis=1, concat_axis=1, tiled=True)  7.33 us
    gather x2, local copies, waits for them, and re-layouts, device_body(): outbound = own_pieces[outgoing_sent_block, outgoing_sent_piece]  5.1 us
    pallas_call x1, Pallas kernels, normalize(): pl.pallas_call(_normalize_kernel, out_shape=jax.ShapeDtypeStruct(source.s...  4.66 us
    ppermute x2, starting transfers between devices, device_body(): arrived_other = lax.ppermute(arrived, 'gy', pair_r)  3.72 us
  transfers between devices with their start and end apart: 8, of which 4 were waited for; matrix products, arithmetic and copies ran while one was open for 25% of the time, Pallas kernels for 0%

profile of v1, /device:TPU:1, one launch (start us, length us, event | category | flops | bytes accessed | tf_op | source)
XLA Modules:
  0.0 130.8 jit_solution(4822628670765998373)
XLA Ops:
  0.0 4.7 %shard_map.46 = bf16[4,512,768]{2,1,0:T(8,128)(2,1)} custom-call(bf16[4,512,768]{2,1,0:T(8,128)(2,1)} %source_ref.1), custom_call_target="tpu_custom_call" | custom-call | flops 4718592 | bytes 6291456 | tf_op jit(solution)/shard_map/pallas_call | solution.py:23
  4.7 2.1 %collective-permute-start.1 = (bf16[4,512,768]{2,1,0:T(8,128)(2,1)}, bf16[4,512,768]{2,1,0:T(8,128)(2,1)}, u32[]{:S(2)}, u32[]{:S(2)}) collective-permute-start(bf16[4,512,768]{2,1,0:T(8,128)(2,1)} %shard_map.46), channel_id=1, source_target_pairs={{0,1},{1,0},{2,3},{3,2},{4,5},{5,4},{6,7},{7,6},{8,9},{9,8},{10,11... | collective-permute-start | bytes 9437192 | tf_op jit(solution)/shard_map/ppermute | solution.py:62
  7.0 3.5 %gather_fusion.1 = bf16[64,8,768]{2,1,0:T(8,128)(2,1)} fusion(bf16[4,64,8,768]{3,2,1,0:T(8,128)(2,1)} %bitcast.173, s32[64]{0:T(128)S(1)} %fusion.63), kind=kCustom, calls=%fused_computation.1 | custom fusion | bytes 1573376 | tf_op jit(solution)/shard_map/gather | solution.py:83
  10.5 12.8 %all-to-all-start = ((bf16[64,8,768]{2,1,0:T(8,128)(2,1)}), bf16[64,8,768]{2,1,0:T(8,128)(2,1)}, u32[]{:S(2)}, u32[]{:S(2)}) async-start(bf16[64,8,768]{2,1,0:T(8,128)(2,1)} %gather_fusion.1), calls=%async_computation | async-start | bytes 1572864 | tf_op jit(solution)/shard_map/all_to_all | solution.py:84
  23.6 0.8 gather_fusion.2
  24.4 0.8 gather_fusion
  25.6 1.6 %gather_fusion.3 = bf16[64,8,768]{2,1,0:T(8,128)(2,1)} fusion(bf16[4,64,8,768]{3,2,1,0:T(8,128)(2,1)S(1)} %bitcast.174, s32[64]{0:T(128)S(1)} %fusion.62), kind=kCustom, calls=%fused_computation.3 | custom fusion | bytes 1573376 | tf_op jit(solution)/shard_map/gather | solution.py:83
  27.6 18.6 %all-to-all-done = bf16[64,8,768]{2,1,0:T(8,128)(2,1)} async-done(((bf16[64,8,768]{2,1,0:T(8,128)(2,1)}), bf16[64,8,768]{2,1,0:T(8,128)(2,1)}, u32[]{:S(2)}, u32[]{:S(2)}) %all-to-all-start) | async-done | bytes 786464 | tf_op jit(solution)/shard_map/all_to_all | solution.py:84
  46.2 6.1 %all-to-all-start.1 = ((bf16[64,8,768]{2,1,0:T(8,128)(2,1)}), bf16[64,8,768]{2,1,0:T(8,128)(2,1)}, u32[]{:S(2)}, u32[]{:S(2)}) async-start(bf16[64,8,768]{2,1,0:T(8,128)(2,1)} %gather_fusion.3), calls=%async_computation.1 | async-start | bytes 1572864 | tf_op jit(solution)/shard_map/all_to_all | solution.py:84
  52.9 1.9 %collective-permute-start = (bf16[64,8,768]{2,1,0:T(8,128)(2,1)}, bf16[64,8,768]{2,1,0:T(8,128)(2,1)}, u32[]{:S(2)}, u32[]{:S(2)}) collective-permute-start(bf16[64,8,768]{2,1,0:T(8,128)(2,1)} %all-to-all-done), channel_id=1, source_target_pairs={{0,3},{1,2},{2,1},{3,0},{4,7},{5,6},{6,5},{7,4},{8,11},{9,10},{10,... | collective-permute-start | bytes 2359304 | tf_op jit(solution)/shard_map/ppermute | solution.py:85
  55.2 20.0 %all-to-all-done.1 = bf16[64,8,768]{2,1,0:T(8,128)(2,1)} async-done(((bf16[64,8,768]{2,1,0:T(8,128)(2,1)}), bf16[64,8,768]{2,1,0:T(8,128)(2,1)}, u32[]{:S(2)}, u32[]{:S(2)}) %all-to-all-start.1) | async-done | bytes 786464 | tf_op jit(solution)/shard_map/all_to_all | solution.py:84
  75.2 1.8 %collective-permute-start.2 = (bf16[64,8,768]{2,1,0:T(8,128)(2,1)}, bf16[64,8,768]{2,1,0:T(8,128)(2,1)S(1)}, u32[]{:S(2)}, u32[]{:S(2)}) collective-permute-start(bf16[64,8,768]{2,1,0:T(8,128)(2,1)} %all-to-all-done.1), channel_id=1, source_target_pairs={{0,3},{1,2},{2,1},{3,0},{4,7},{5,6},{6,5},{7,4},{8,11},{9,10},{10,... | collective-permute-start | bytes 2359304 | tf_op jit(solution)/shard_map/ppermute | solution.py:85
  77.0 3.5 %fusion = (f32[4,512]{1,0:T(4,128)S(1)}, f32[64,8]{1,0:T(8,128)S(1)}) fusion(pred[4,512]{1,0:T(4,128)(4,1)S(1)} %iota_compare_fusion.5, pred[64,8,4]{1,2,0:T(4,128)(4,1)S(1)} %get-tuple-element.60, bf16[4,512,768]{2,1,0:T(8,128)(2,1)S(1)} %copy-done.1, bf16[64,8,768]{2,1,0:T(8,128)(2,1)} %all-to-all-done), kind=kOutput, calls=%fused_computation.12 | convolution fusion | flops 1614804480 | bytes 3946496 | tf_op jit(solution)/shard_map/rd,kcd->rkc/dot_general | solution.py:40
  80.5 3.5 %fusion.6 = (f32[4,512]{1,0:T(4,128)S(1)}, f32[64,8]{1,0:T(8,128)S(1)}) fusion(pred[64,8,4]{1,2,0:T(4,128)(4,1)S(1)} %get-tuple-element.59, pred[4,512]{1,0:T(4,128)(4,1)S(1)} %iota_compare_fusion.5, bf16[4,512,768]{2,1,0:T(8,128)(2,1)S(1)} %copy-done.1, bf16[64,8,768]{2,1,0:T(8,128)(2,1)} %collective-permute-done), kind=kOutput, calls=%fused_computation.18 | convolution fusion | flops 1614804480 | bytes 3946496 | tf_op jit(solution)/shard_map/rd,kcd->rkc/dot_general | solution.py:40
  84.0 3.5 %fusion.4 = (f32[4,512]{1,0:T(4,128)S(1)}, f32[64,8]{1,0:T(8,128)S(1)}) fusion(pred[64,8,4]{1,2,0:T(4,128)(4,1)S(1)} %get-tuple-element.58, pred[4,512]{1,0:T(4,128)(4,1)S(1)} %iota_compare_fusion.5, bf16[4,512,768]{2,1,0:T(8,128)(2,1)S(1)} %copy-done.1, bf16[64,8,768]{2,1,0:T(8,128)(2,1)} %all-to-all-done.1), kind=kOutput, calls=%fused_computation.16 | convolution fusion | flops 1614804480 | bytes 3946496 | tf_op jit(solution)/shard_map/rd,kcd->rkc/dot_general | solution.py:40
  87.5 4.2 %fusion.2 = (f32[4,512]{1,0:T(4,128)S(1)}, f32[64,8]{1,0:T(8,128)S(1)}) fusion(pred[4,512]{1,0:T(4,128)(4,1)S(1)} %iota_compare_fusion.4, pred[64,8,4]{1,2,0:T(4,128)(4,1)S(1)} %get-tuple-element.60, bf16[4,512,768]{2,1,0:T(8,128)(2,1)} %collective-permute-done.1, bf16[64,8,768]{2,1,0:T(8,128)(2,1)} %all-to-all-done), kind=kOutput, calls=%fused_computation.14 | convolution fusion | flops 1614804480 | bytes 3946496 | tf_op jit(solution)/shard_map/rd,kcd->rkc/dot_general | solution.py:40
  91.6 4.2 %fusion.10 = (f32[4,512]{1,0:T(4,128)S(1)}, f32[64,8]{1,0:T(8,128)S(1)}) fusion(pred[64,8,4]{1,2,0:T(4,128)(4,1)S(1)} %get-tuple-element.59, pred[4,512]{1,0:T(4,128)(4,1)S(1)} %iota_compare_fusion.4, bf16[4,512,768]{2,1,0:T(8,128)(2,1)} %collective-permute-done.1, bf16[64,8,768]{2,1,0:T(8,128)(2,1)} %collective-permute-done), kind=kOutput, calls=%fused_computation.22 | convolution fusion | flops 1614804480 | bytes 3946496 | tf_op jit(solution)/shard_map/rd,kcd->rkc/dot_general | solution.py:40
  95.8 4.2 %fusion.8 = (f32[4,512]{1,0:T(4,128)S(1)}, f32[64,8]{1,0:T(8,128)S(1)}) fusion(pred[64,8,4]{1,2,0:T(4,128)(4,1)S(1)} %get-tuple-element.58, pred[4,512]{1,0:T(4,128)(4,1)S(1)} %iota_compare_fusion.4, bf16[4,512,768]{2,1,0:T(8,128)(2,1)} %collective-permute-done.1, bf16[64,8,768]{2,1,0:T(8,128)(2,1)} %all-to-all-done.1), kind=kOutput, calls=%fused_computation.20 | convolution fusion | flops 1614804480 | bytes 3946496 | tf_op jit(solution)/shard_map/rd,kcd->rkc/dot_general | solution.py:40
  100.0 2.3 %fusion.12 = (f32[4,512]{1,0:T(4,128)S(1)}, f32[64,8]{1,0:T(8,128)S(1)}) fusion(pred[64,8,4]{1,2,0:T(4,128)(4,1)S(1)} %get-tuple-element.57, pred[4,512]{1,0:T(4,128)(4,1)S(1)} %iota_compare_fusion.5, bf16[4,512,768]{2,1,0:T(8,128)(2,1)S(1)} %copy-done.1, bf16[64,8,768]{2,1,0:T(8,128)(2,1)S(1)} %collective-permute-done.2), kind=kOutput, calls=%fused_computation.24 | convolution fusion | flops 1614804480 | bytes 3946496 | tf_op jit(solution)/shard_map/rd,kcd->rkc/dot_general | solution.py:40
  102.4 4.5 %fusion.14 = (f32[4,512]{1,0:T(4,128)S(1)}, f32[64,8]{1,0:T(8,128)S(1)}) fusion(pred[64,8,4]{1,2,0:T(4,128)(4,1)S(1)} %get-tuple-element.57, pred[4,512]{1,0:T(4,128)(4,1)S(1)} %iota_compare_fusion.4, bf16[4,512,768]{2,1,0:T(8,128)(2,1)} %collective-permute-done.1, bf16[64,8,768]{2,1,0:T(8,128)(2,1)S(1)} %collective-permute-done.2), kind=kOutput, calls=%fused_computation.26 | convolution fusion | flops 1614804480 | bytes 3946496 | tf_op jit(solution)/shard_map/rd,kcd->rkc/dot_general | solution.py:40
  106.9 0.9 collective-permute-start.3
  107.8 3.5 %collective-permute-done.3 = f32[2,64,8]{2,1,0:T(8,128)S(1)} collective-permute-done((f32[2,64,8]{2,1,0:T(8,128)S(1)}, f32[2,64,8]{2,1,0:T(8,128)S(1)}, u32[]{:S(2)}, u32[]{:S(2)}) %collective-permute-start.3) | collective-permute-done | bytes 4128 | tf_op jit(solution)/shard_map/ppermute | solution.py:115
  112.0 7.3 %all-to-all-start.2 = ((f32[2,64,8]{2,0,1:T(2,128)}), f32[2,64,8]{2,0,1:T(2,128)S(1)}, u32[]{:S(2)}, u32[]{:S(2)}) async-start(f32[2,64,8]{2,0,1:T(2,128)} %copy.31), calls=%async_computation.2 | async-start | bytes 131072 | tf_op jit(solution)/shard_map/all_to_all | solution.py:117
  119.4 10.0 %all-to-all-done.2 = f32[2,64,8]{2,0,1:T(2,128)S(1)} async-done(((f32[2,64,8]{2,0,1:T(2,128)}), f32[2,64,8]{2,0,1:T(2,128)S(1)}, u32[]{:S(2)}, u32[]{:S(2)}) %all-to-all-start.2) | async-done | bytes 4128 | tf_op jit(solution)/shard_map/all_to_all | solution.py:117
  (64 shorter events, 4.5 us)
Async XLA Ops:
  0.0 6.8 %copy-start.3 = (s32[2,64,64]{2,1,0:T(8,128)S(1)}, s32[2,64,64]{2,1,0:T(8,128)}, u32[]{:S(2)}) copy-start(s32[2,64,64]{2,1,0:T(8,128)} %param.5) | copy-start | bytes 98308
  4.7 18.9 %copy-start = (s32[256]{0:T(256)S(1)}, s32[256]{0:T(256)}, u32[]{:S(2)}) copy-start(s32[256]{0:T(256)} %param.7) | copy-start | bytes 3076
  4.7 20.6 %copy-start.2 = (s32[2,64,64,2]{2,3,1,0:T(2,128)S(1)}, s32[2,64,64,2]{2,3,1,0:T(2,128)}, u32[]{:S(2)}) copy-start(s32[2,64,64,2]{2,3,1,0:T(2,128)} %param.6) | copy-start | bytes 196612
  4.7 20.9 %copy-start.1 = (bf16[4,512,768]{2,1,0:T(8,128)(2,1)S(1)}, bf16[4,512,768]{2,1,0:T(8,128)(2,1)}, u32[]{:S(2)}) copy-start(bf16[4,512,768]{2,1,0:T(8,128)(2,1)} %shard_map.46) | copy-start | bytes 9437188
  4.7 82.8 %collective-permute-start.1 = (bf16[4,512,768]{2,1,0:T(8,128)(2,1)}, bf16[4,512,768]{2,1,0:T(8,128)(2,1)}, u32[]{:S(2)}, u32[]{:S(2)}) collective-permute-start(bf16[4,512,768]{2,1,0:T(8,128)(2,1)} %shard_map.46), channel_id=1, source_target_pairs={{0,1},{1,0},{2,3},{3,2},{4,5},{5,4},{6,7},{7,6},{8,9},{9,8},{10,11... | collective-permute-start | bytes 9437192 | tf_op jit(solution)/shard_map/ppermute | solution.py:62
  10.5 35.7 %all-to-all-start = ((bf16[64,8,768]{2,1,0:T(8,128)(2,1)}), bf16[64,8,768]{2,1,0:T(8,128)(2,1)}, u32[]{:S(2)}, u32[]{:S(2)}) async-start(bf16[64,8,768]{2,1,0:T(8,128)(2,1)} %gather_fusion.1), calls=%async_computation | async-start | bytes 1572864 | tf_op jit(solution)/shard_map/all_to_all | solution.py:84
  46.2 29.0 %all-to-all-start.1 = ((bf16[64,8,768]{2,1,0:T(8,128)(2,1)}), bf16[64,8,768]{2,1,0:T(8,128)(2,1)}, u32[]{:S(2)}, u32[]{:S(2)}) async-start(bf16[64,8,768]{2,1,0:T(8,128)(2,1)} %gather_fusion.3), calls=%async_computation.1 | async-start | bytes 1572864 | tf_op jit(solution)/shard_map/all_to_all | solution.py:84
  52.9 27.6 %collective-permute-start = (bf16[64,8,768]{2,1,0:T(8,128)(2,1)}, bf16[64,8,768]{2,1,0:T(8,128)(2,1)}, u32[]{:S(2)}, u32[]{:S(2)}) collective-permute-start(bf16[64,8,768]{2,1,0:T(8,128)(2,1)} %all-to-all-done), channel_id=1, source_target_pairs={{0,3},{1,2},{2,1},{3,0},{4,7},{5,6},{6,5},{7,4},{8,11},{9,10},{10,... | collective-permute-start | bytes 2359304 | tf_op jit(solution)/shard_map/ppermute | solution.py:85
  75.2 24.8 %collective-permute-start.2 = (bf16[64,8,768]{2,1,0:T(8,128)(2,1)}, bf16[64,8,768]{2,1,0:T(8,128)(2,1)S(1)}, u32[]{:S(2)}, u32[]{:S(2)}) collective-permute-start(bf16[64,8,768]{2,1,0:T(8,128)(2,1)} %all-to-all-done.1), channel_id=1, source_target_pairs={{0,3},{1,2},{2,1},{3,0},{4,7},{5,6},{6,5},{7,4},{8,11},{9,10},{10,... | collective-permute-start | bytes 2359304 | tf_op jit(solution)/shard_map/ppermute | solution.py:85
  106.9 4.4 %collective-permute-start.3 = (f32[2,64,8]{2,1,0:T(8,128)S(1)}, f32[2,64,8]{2,1,0:T(8,128)S(1)}, u32[]{:S(2)}, u32[]{:S(2)}) collective-permute-start(f32[2,64,8]{2,1,0:T(8,128)S(1)} %pad_maximum_fusion), channel_id=1, source_target_pairs={{0,3},{1,2},{2,1},{3,0},{4,7},{5,6},{6,5},{7,4},{8,11},{9,10},{10,... | collective-permute-start | bytes 12296 | tf_op jit(solution)/shard_map/ppermute | solution.py:115
  112.0 17.4 %all-to-all-start.2 = ((f32[2,64,8]{2,0,1:T(2,128)}), f32[2,64,8]{2,0,1:T(2,128)S(1)}, u32[]{:S(2)}, u32[]{:S(2)}) async-start(f32[2,64,8]{2,0,1:T(2,128)} %copy.31), calls=%async_computation.2 | async-start | bytes 131072 | tf_op jit(solution)/shard_map/all_to_all | solution.py:117
  119.3 10.8 %collective-permute-start.4 = (f32[4,512]{1,0:T(4,128)S(1)}, f32[4,512]{1,0:T(4,128)S(1)}, u32[]{:S(2)}, u32[]{:S(2)}) collective-permute-start(f32[4,512]{1,0:T(4,128)S(1)} %maximum_maximum_fusion.2), channel_id=1, source_target_pairs={{0,1},{1,0},{2,3},{3,2},{4,5},{5,4},{6,7},{7,6},{8,9},{9,8},{10,11... | collective-permute-start | bytes 24584 | tf_op jit(solution)/shard_map/ppermute | solution.py:112

commit v2 on v0

--- a/solution.py
+++ b/solution.py
@@ -66,33 +66,49 @@
         sent_pieces.append(outgoing_sent_piece)
         outbound = own_pieces[outgoing_sent_block, outgoing_sent_piece]
         arrived = lax.all_to_all(outbound, "gx", split_axis=0, concat_axis=0, tiled=True)
-        arrived_other = lax.ppermute(arrived, "gy", pair_r)
+        halves = 2 if wave_index == waves - 1 else 1
+        span = arrived.shape[0] // halves
+        arrived_other = []
+        for half in range(halves):
+            piece = arrived[half * span : (half + 1) * span]
+            arrived_other.append(lax.ppermute(piece, "gy", pair_r))
         incoming = lax.dynamic_index_in_dim(fetch_list[wave_index], my_group, 0, False)
         arrived_counts = counts[incoming // pieces]
         chosen = lax.dynamic_index_in_dim(partners[wave_index], my_group, 0, False) - first
         listed = jnp.any(chosen[:, :, None] == local_ids[None, None, :], axis=1)
         piece_rows = (incoming % pieces)[:, None] * slice_rows + slice_offsets[None, :]
-        for part, (lane, rows_in) in enumerate(((my_lane, arrived), (lane_r, arrived_other))):
-            row_valid = (lane * quarter + piece_rows) < arrived_counts[:, None]
-            jobs.append((wave_index, part, rows_in, row_valid, listed))
+        row_valid = (my_lane * quarter + piece_rows) < arrived_counts[:, None]
+        jobs.append((wave_index, 0, 0, arrived, row_valid, listed))
+        row_valid = (lane_r * quarter + piece_rows) < arrived_counts[:, None]
+        for half, rows_in in enumerate(arrived_other):
+            cut = slice(half * span, (half + 1) * span)
+            jobs.append((wave_index, 1, half, rows_in, row_valid[cut], listed[cut]))
     row_best = {}
     token = None
     order = sorted(
         ((source, job) for source in range(len(col_sources)) for job in range(len(jobs))),
-        key=lambda item: (jobs[item[1]][0] == waves - 1 and jobs[item[1]][1] == 1, item[0], item[1]),
+        key=lambda item: (
+            jobs[item[1]][0] == waves - 1 and jobs[item[1]][1] == 1,
+            jobs[item[1]][2],
+            item[0],
+            item[1],
+        ),
     )
     for source, job in order:
         unit, col_limit = col_sources[source]
-        wave_index, part, rows_in, row_valid, listed = jobs[job]
+        wave_index, part, half, rows_in, row_valid, listed = jobs[job]
         if token is not None:
             token, rows_in, unit = lax.optimization_barrier((token, rows_in, unit))
         rows_max, col_best = lent_scores(rows_in, row_valid, listed, unit, col_limit)
         token = (rows_max, col_best)
-        key = (wave_index, part)
+        key = (wave_index, part, half)
         row_best[key] = rows_max if key not in row_best else jnp.maximum(row_best[key], rows_max)
         col_part[source] = jnp.maximum(col_part[source], col_best)
-    row_mine_parts = [row_best[(wave_index, 0)] for wave_index in range(waves)]
-    row_other_parts = [row_best[(wave_index, 1)] for wave_index in range(waves)]
+    row_mine_parts = [row_best[(wave_index, 0, 0)] for wave_index in range(waves)]
+    row_other_parts = []
+    for wave_index in range(waves):
+        pieces_of = sorted(k for k in row_best if k[0] == wave_index and k[1] == 1)
+        row_other_parts.append(jnp.concatenate([row_best[k] for k in pieces_of], axis=0))
     col_back = lax.ppermute(col_part[1], "gy", pair_p)
     col_total = jnp.maximum(col_part[0], col_back)
     row_other = jnp.stack(row_other_parts, axis=0)

time: 146 us -> 150 us (1.027)
  matrix products: 35 us -> 38.5 us
    dot_general x8 -> x10, matrix products: 35 us -> 38.5 us  [lent_scores(): jnp.einsum('rd,kcd->rkc', flat_rows, columns, preferred_element_type=jnp....]
    ppermute x2 -> x3, starting transfers between devices: 5.04 us -> 5.33 us  [device_body(): arrived_other.append(lax.ppermute(piece, 'gy', pair_r))]
  transfers between devices with their start and end apart: 8 -> 9, of which waited for: 5 -> 5; matrix products, arithmetic and copies ran while one was open for 25% -> 29% of each run, Pallas kernels for 0% -> 0%
where the time goes in v2:
time: 150 us; the launch traced here: 149 us
  waiting for transfers between devices  47.6 us (32%)
  starting transfers between devices  40.8 us (27%)
  matrix products  38.5 us (26%)
  local copies, waits for them, and re-layouts  12 us (8%)
  other arithmetic  9.82 us (7%)
    dot_general x10, matrix products, lent_scores(): jnp.einsum('rd,kcd->rkc', flat_rows, columns, preferred_element_type=jnp....  38.5 us
    all_to_all x2, waiting for transfers between devices, device_body(): lax.all_to_all(outbound, 'gx', split_axis=0, concat_axis=0, tiled=True)  32 us
    all_to_all x2, starting transfers between devices, device_body(): lax.all_to_all(outbound, 'gx', split_axis=0, concat_axis=0, tiled=True)  19.2 us
    all_to_all x1, starting transfers between devices, device_body(): lax.all_to_all(row_mine, 'gx', split_axis=1, concat_axis=1, tiled=True)  12.4 us
    all_to_all x1, waiting for transfers between devices, device_body(): lax.all_to_all(row_mine, 'gx', split_axis=1, concat_axis=1, tiled=True)  9.97 us
    gather x2, local copies, waits for them, and re-layouts, device_body(): outbound = own_pieces[outgoing_sent_block, outgoing_sent_piece]  7 us
    ppermute x3, starting transfers between devices, device_body(): arrived_other.append(lax.ppermute(piece, 'gy', pair_r))  5.33 us
    ppermute x1, waiting for transfers between devices, device_body(): other_unit = lax.ppermute(own_unit, 'gy', pair_p)  3.79 us
  transfers between devices with their start and end apart: 9, of which 5 were waited for; matrix products, arithmetic and copies ran while one was open for 29% of the time, Pallas kernels for 0%

profile of v2, /device:TPU:1, one launch (start us, length us, event | category | flops | bytes accessed | tf_op | source)
XLA Modules:
  0.0 149.1 jit_solution(11210109078442177490)
XLA Ops:
  0.9 2.6 %fusion = f32[4,512]{1,0:T(4,128)S(1)} fusion(bf16[4,512,768]{2,1,0:T(8,128)(2,1)} %param.4), kind=kLoop, calls=%fused_computation.6 | loop fusion | flops 4716544 | bytes 3153920 | tf_op jit(solution)/shard_map/reduce_sum | solution.py:15
  3.6 2.3 %fusion.84 = bf16[4,64,8,768]{3,2,1,0:T(8,128)(2,1)} fusion(f32[4,512]{1,0:T(4,128)S(1)} %add_rsqrt_fusion, bf16[4,512,768]{2,1,0:T(8,128)(2,1)S(1)} %copy-done.1), kind=kLoop, calls=%fused_computation.188 | loop fusion | flops 4718592 | bytes 6299648 | tf_op jit(solution)/shard_map/reshape | solution.py:47
  6.1 3.5 %gather_fusion.1 = bf16[64,8,768]{2,1,0:T(8,128)(2,1)} fusion(bf16[4,64,8,768]{3,2,1,0:T(8,128)(2,1)} %fusion.84, s32[64]{0:T(128)S(1)} %fusion.75), kind=kCustom, calls=%fused_computation.1 | custom fusion | bytes 1573376 | tf_op jit(solution)/shard_map/gather | solution.py:67
  9.6 13.3 %all-to-all-start = ((bf16[64,8,768]{2,1,0:T(8,128)(2,1)}), bf16[64,8,768]{2,1,0:T(8,128)(2,1)}, u32[]{:S(2)}, u32[]{:S(2)}) async-start(bf16[64,8,768]{2,1,0:T(8,128)(2,1)} %gather_fusion.1), calls=%async_computation | async-start | bytes 1572864 | tf_op jit(solution)/shard_map/all_to_all | solution.py:68
  28.3 3.5 %gather_fusion.3 = bf16[64,8,768]{2,1,0:T(8,128)(2,1)} fusion(bf16[4,64,8,768]{3,2,1,0:T(8,128)(2,1)} %fusion.84, s32[64]{0:T(128)S(1)} %fusion.74), kind=kCustom, calls=%fused_computation.3 | custom fusion | bytes 1573376 | tf_op jit(solution)/shard_map/gather | solution.py:67
  32.8 13.1 %all-to-all-done = bf16[64,8,768]{2,1,0:T(8,128)(2,1)} async-done(((bf16[64,8,768]{2,1,0:T(8,128)(2,1)}), bf16[64,8,768]{2,1,0:T(8,128)(2,1)}, u32[]{:S(2)}, u32[]{:S(2)}) %all-to-all-start) | async-done | bytes 786464 | tf_op jit(solution)/shard_map/all_to_all | solution.py:68
  45.8 5.9 %all-to-all-start.1 = ((bf16[64,8,768]{2,1,0:T(8,128)(2,1)}), bf16[64,8,768]{2,1,0:T(8,128)(2,1)S(1)}, u32[]{:S(2)}, u32[]{:S(2)}) async-start(bf16[64,8,768]{2,1,0:T(8,128)(2,1)} %gather_fusion.3), calls=%async_computation.1 | async-start | bytes 1572864 | tf_op jit(solution)/shard_map/all_to_all | solution.py:68
  53.2 2.6 %collective-permute-start = (bf16[64,8,768]{2,1,0:T(8,128)(2,1)}, bf16[64,8,768]{2,1,0:T(8,128)(2,1)S(1)}, u32[]{:S(2)}, u32[]{:S(2)}) collective-permute-start(bf16[64,8,768]{2,1,0:T(8,128)(2,1)} %all-to-all-done), channel_id=1, source_target_pairs={{0,3},{1,2},{2,1},{3,0},{4,7},{5,6},{6,5},{7,4},{8,11},{9,10},{10,... | collective-permute-start | bytes 2359304 | tf_op jit(solution)/shard_map/ppermute | solution.py:74
  55.8 18.9 %all-to-all-done.1 = bf16[64,8,768]{2,1,0:T(8,128)(2,1)S(1)} async-done(((bf16[64,8,768]{2,1,0:T(8,128)(2,1)}), bf16[64,8,768]{2,1,0:T(8,128)(2,1)S(1)}, u32[]{:S(2)}, u32[]{:S(2)}) %all-to-all-start.1) | async-done | bytes 786464 | tf_op jit(solution)/shard_map/all_to_all | solution.py:68
  74.8 2.6 %collective-permute-start.2 = (bf16[32,8,768]{2,1,0:T(8,128)(2,1)S(1)}, bf16[32,8,768]{2,1,0:T(8,128)(2,1)S(1)}, u32[]{:S(2)}, u32[]{:S(2)}) collective-permute-start(bf16[32,8,768]{2,1,0:T(8,128)(2,1)S(1)} %get-tuple-element.64), channel_id=1, source_target_pairs={{0,3},{1,2},{2,1},{3,0},{4,7},{5,6},{6,5},{7,4},{8,11},{9,10},{10,... | collective-permute-start | bytes 1179656 | tf_op jit(solution)/shard_map/ppermute | solution.py:74
  77.6 4.2 %fusion.2 = (f32[4,512]{1,0:T(4,128)S(1)}, f32[64,8]{1,0:T(8,128)S(1)}) fusion(pred[4,512]{1,0:T(4,128)(4,1)S(1)} %iota_compare_fusion.5, pred[64,8,4]{1,2,0:T(4,128)(4,1)S(1)} %get-tuple-element.72, bf16[4,512,768]{2,1,0:T(8,128)(2,1)} %fusion.1, bf16[64,8,768]{2,1,0:T(8,128)(2,1)} %all-to-all-done), kind=kOutput, calls=%fused_computation.14 | convolution fusion | flops 1614804480 | bytes 3946496 | tf_op jit(solution)/shard_map/rd,kcd->rkc/dot_general | solution.py:24
  81.7 4.6 %fusion.8 = (f32[4,512]{1,0:T(4,128)S(1)}, f32[64,8]{1,0:T(8,128)S(1)}) fusion(pred[64,8,4]{1,2,0:T(4,128)(4,1)S(1)} %get-tuple-element.71, pred[4,512]{1,0:T(4,128)(4,1)S(1)} %iota_compare_fusion.5, bf16[4,512,768]{2,1,0:T(8,128)(2,1)} %fusion.1, bf16[64,8,768]{2,1,0:T(8,128)(2,1)S(1)} %collective-permute-done), kind=kOutput, calls=%fused_computation.20 | convolution fusion | flops 1614804480 | bytes 3946496 | tf_op jit(solution)/shard_map/rd,kcd->rkc/dot_general | solution.py:24
  86.4 4.4 %fusion.6 = (f32[4,512]{1,0:T(4,128)S(1)}, f32[64,8]{1,0:T(8,128)S(1)}) fusion(pred[64,8,4]{1,2,0:T(4,128)(4,1)S(1)} %broadcast_and_fusion.2, pred[4,512]{1,0:T(4,128)(4,1)S(1)} %iota_compare_fusion.5, bf16[4,512,768]{2,1,0:T(8,128)(2,1)} %fusion.1, bf16[64,8,768]{2,1,0:T(8,128)(2,1)S(1)} %all-to-all-done.1), kind=kOutput, calls=%fused_computation.18 | convolution fusion | flops 1614804480 | bytes 3946496 | tf_op jit(solution)/shard_map/rd,kcd->rkc/dot_general | solution.py:24
  90.8 3.8 %collective-permute-done.1 = bf16[4,512,768]{2,1,0:T(8,128)(2,1)} collective-permute-done((bf16[4,512,768]{2,1,0:T(8,128)(2,1)}, bf16[4,512,768]{2,1,0:T(8,128)(2,1)}, u32[]{:S(2)}, u32[]{:S(2)}) %collective-permute-start.1) | collective-permute-done | bytes 3145760 | tf_op jit(solution)/shard_map/ppermute | solution.py:46
  94.6 4.2 %fusion.4 = (f32[4,512]{1,0:T(4,128)S(1)}, f32[64,8]{1,0:T(8,128)S(1)}) fusion(pred[4,512]{1,0:T(4,128)(4,1)S(1)} %iota_compare_fusion.4, pred[64,8,4]{1,2,0:T(4,128)(4,1)S(1)} %get-tuple-element.72, bf16[4,512,768]{2,1,0:T(8,128)(2,1)} %collective-permute-done.1, bf16[64,8,768]{2,1,0:T(8,128)(2,1)} %all-to-all-done), kind=kOutput, calls=%fused_computation.16 | convolution fusion | flops 1614804480 | bytes 3946496 | tf_op jit(solution)/shard_map/rd,kcd->rkc/dot_general | solution.py:24
  98.8 4.5 %fusion.12 = (f32[4,512]{1,0:T(4,128)S(1)}, f32[64,8]{1,0:T(8,128)S(1)}) fusion(pred[64,8,4]{1,2,0:T(4,128)(4,1)S(1)} %get-tuple-element.71, pred[4,512]{1,0:T(4,128)(4,1)S(1)} %iota_compare_fusion.4, bf16[4,512,768]{2,1,0:T(8,128)(2,1)} %collective-permute-done.1, bf16[64,8,768]{2,1,0:T(8,128)(2,1)S(1)} %collective-permute-done), kind=kOutput, calls=%fused_computation.24 | convolution fusion | flops 1614804480 | bytes 3946496 | tf_op jit(solution)/shard_map/rd,kcd->rkc/dot_general | solution.py:24
  103.2 4.4 %fusion.10 = (f32[4,512]{1,0:T(4,128)S(1)}, f32[64,8]{1,0:T(8,128)S(1)}) fusion(pred[64,8,4]{1,2,0:T(4,128)(4,1)S(1)} %broadcast_and_fusion.2, pred[4,512]{1,0:T(4,128)(4,1)S(1)} %iota_compare_fusion.4, bf16[4,512,768]{2,1,0:T(8,128)(2,1)} %collective-permute-done.1, bf16[64,8,768]{2,1,0:T(8,128)(2,1)S(1)} %all-to-all-done.1), kind=kOutput, calls=%fused_computation.22 | convolution fusion | flops 1614804480 | bytes 3946496 | tf_op jit(solution)/shard_map/rd,kcd->rkc/dot_general | solution.py:24
  107.7 3.1 %fusion.34 = (f32[4,512]{1,0:T(4,128)S(1)}, f32[32,8]{1,0:T(8,128)S(1)}) fusion(pred[4,512]{1,0:T(4,128)(4,1)S(1)} %iota_compare_fusion.5, pred[32,8,4]{1,2,0:T(4,128)(4,1)S(1)} %broadcast_and_fusion.6, bf16[4,512,768]{2,1,0:T(8,128)(2,1)} %fusion.1, bf16[32,8,768]{2,1,0:T(8,128)(2,1)S(1)} %collective-permute-done.2), kind=kOutput, calls=%fused_computation.50 | convolution fusion | flops 807401216 | bytes 3551232 | tf_op jit(solution)/shard_map/rd,kcd->rkc/dot_general | solution.py:24
  110.7 3.1 %fusion.36 = (f32[4,512]{1,0:T(4,128)S(1)}, f32[32,8]{1,0:T(8,128)S(1)}) fusion(pred[4,512]{1,0:T(4,128)(4,1)S(1)} %iota_compare_fusion.4, pred[32,8,4]{1,2,0:T(4,128)(4,1)S(1)} %broadcast_and_fusion.6, bf16[4,512,768]{2,1,0:T(8,128)(2,1)} %collective-permute-done.1, bf16[32,8,768]{2,1,0:T(8,128)(2,1)S(1)} %collective-permute-done.2), kind=kOutput, calls=%fused_computation.52 | convolution fusion | flops 807401216 | bytes 3551232 | tf_op jit(solution)/shard_map/rd,kcd->rkc/dot_general | solution.py:24
  113.9 3.1 %fusion.38 = (f32[4,512]{1,0:T(4,128)S(1)}, f32[32,8]{1,0:T(8,128)S(1)}) fusion(pred[32,8,4]{1,2,0:T(4,128)(4,1)S(1)} %broadcast_and_fusion.5, pred[4,512]{1,0:T(4,128)(4,1)S(1)} %iota_compare_fusion.5, bf16[4,512,768]{2,1,0:T(8,128)(2,1)} %fusion.1, bf16[32,8,768]{2,1,0:T(8,128)(2,1)S(1)} %collective-permute-done.3), kind=kOutput, calls=%fused_computation.54 | convolution fusion | flops 807401216 | bytes 3551232 | tf_op jit(solution)/shard_map/rd,kcd->rkc/dot_general | solution.py:24
  116.9 3.1 %fusion.40 = (f32[4,512]{1,0:T(4,128)S(1)}, f32[32,8]{1,0:T(8,128)S(1)}) fusion(pred[32,8,4]{1,2,0:T(4,128)(4,1)S(1)} %broadcast_and_fusion.5, pred[4,512]{1,0:T(4,128)(4,1)S(1)} %iota_compare_fusion.4, bf16[4,512,768]{2,1,0:T(8,128)(2,1)} %collective-permute-done.1, bf16[32,8,768]{2,1,0:T(8,128)(2,1)S(1)} %collective-permute-done.3), kind=kOutput, calls=%fused_computation.56 | convolution fusion | flops 807401216 | bytes 3551232 | tf_op jit(solution)/shard_map/rd,kcd->rkc/dot_general | solution.py:24
  120.0 2.6 %collective-permute-start.4 = (f32[2,64,8]{2,1,0:T(8,128)S(1)}, f32[2,64,8]{2,1,0:T(8,128)S(1)}, u32[]{:S(2)}, u32[]{:S(2)}) collective-permute-start(f32[2,64,8]{2,1,0:T(8,128)S(1)} %pad_maximum_fusion), channel_id=1, source_target_pairs={{0,3},{1,2},{2,1},{3,0},{4,7},{5,6},{6,5},{7,4},{8,11},{9,10},{10,... | collective-permute-start | bytes 12296 | tf_op jit(solution)/shard_map/ppermute | solution.py:115
  125.1 12.4 %all-to-all-start.2 = ((f32[2,64,8]{2,0,1:T(2,128)}), f32[2,64,8]{2,0,1:T(2,128)S(1)}, u32[]{:S(2)}, u32[]{:S(2)}) async-start(f32[2,64,8]{2,0,1:T(2,128)} %copy.46), calls=%async_computation.2 | async-start | bytes 131072 | tf_op jit(solution)/shard_map/all_to_all | solution.py:117
  137.7 10.0 %all-to-all-done.2 = f32[2,64,8]{2,0,1:T(2,128)S(1)} async-done(((f32[2,64,8]{2,0,1:T(2,128)}), f32[2,64,8]{2,0,1:T(2,128)S(1)}, u32[]{:S(2)}, u32[]{:S(2)}) %all-to-all-start.2) | async-done | bytes 4128 | tf_op jit(solution)/shard_map/all_to_all | solution.py:117
  (79 shorter events, 13.2 us)
Async XLA Ops:
  0.0 3.6 %copy-start.1 = (bf16[4,512,768]{2,1,0:T(8,128)(2,1)S(1)}, bf16[4,512,768]{2,1,0:T(8,128)(2,1)}, u32[]{:S(2)}) copy-start(bf16[4,512,768]{2,1,0:T(8,128)(2,1)} %param.4) | copy-start | bytes 9437188
  9.6 36.3 %all-to-all-start = ((bf16[64,8,768]{2,1,0:T(8,128)(2,1)}), bf16[64,8,768]{2,1,0:T(8,128)(2,1)}, u32[]{:S(2)}, u32[]{:S(2)}) async-start(bf16[64,8,768]{2,1,0:T(8,128)(2,1)} %gather_fusion.1), calls=%async_computation | async-start | bytes 1572864 | tf_op jit(solution)/shard_map/all_to_all | solution.py:68
  22.9 3.8 %copy-start = (s32[256]{0:T(256)S(1)}, s32[256]{0:T(256)}, u32[]{:S(2)}) copy-start(s32[256]{0:T(256)} %param.7) | copy-start | bytes 3076
  22.9 5.4 %copy-start.2 = (s32[2,64,64,2]{2,3,1,0:T(2,128)S(1)}, s32[2,64,64,2]{2,3,1,0:T(2,128)}, u32[]{:S(2)}) copy-start(s32[2,64,64,2]{2,3,1,0:T(2,128)} %param.6) | copy-start | bytes 196612
  25.2 69.5 %collective-permute-start.1 = (bf16[4,512,768]{2,1,0:T(8,128)(2,1)}, bf16[4,512,768]{2,1,0:T(8,128)(2,1)}, u32[]{:S(2)}, u32[]{:S(2)}) collective-permute-start(bf16[4,512,768]{2,1,0:T(8,128)(2,1)} %fusion.1), channel_id=1, source_target_pairs={{0,1},{1,0},{2,3},{3,2},{4,5},{5,4},{6,7},{7,6},{8,9},{9,8},{10,11... | collective-permute-start | bytes 9437192 | tf_op jit(solution)/shard_map/ppermute | solution.py:46
  45.8 28.9 %all-to-all-start.1 = ((bf16[64,8,768]{2,1,0:T(8,128)(2,1)}), bf16[64,8,768]{2,1,0:T(8,128)(2,1)S(1)}, u32[]{:S(2)}, u32[]{:S(2)}) async-start(bf16[64,8,768]{2,1,0:T(8,128)(2,1)} %gather_fusion.3), calls=%async_computation.1 | async-start | bytes 1572864 | tf_op jit(solution)/shard_map/all_to_all | solution.py:68
  53.2 28.5 %collective-permute-start = (bf16[64,8,768]{2,1,0:T(8,128)(2,1)}, bf16[64,8,768]{2,1,0:T(8,128)(2,1)S(1)}, u32[]{:S(2)}, u32[]{:S(2)}) collective-permute-start(bf16[64,8,768]{2,1,0:T(8,128)(2,1)} %all-to-all-done), channel_id=1, source_target_pairs={{0,3},{1,2},{2,1},{3,0},{4,7},{5,6},{6,5},{7,4},{8,11},{9,10},{10,... | collective-permute-start | bytes 2359304 | tf_op jit(solution)/shard_map/ppermute | solution.py:74
  74.8 32.9 %collective-permute-start.2 = (bf16[32,8,768]{2,1,0:T(8,128)(2,1)S(1)}, bf16[32,8,768]{2,1,0:T(8,128)(2,1)S(1)}, u32[]{:S(2)}, u32[]{:S(2)}) collective-permute-start(bf16[32,8,768]{2,1,0:T(8,128)(2,1)S(1)} %get-tuple-element.64), channel_id=1, source_target_pairs={{0,3},{1,2},{2,1},{3,0},{4,7},{5,6},{6,5},{7,4},{8,11},{9,10},{10,... | collective-permute-start | bytes 1179656 | tf_op jit(solution)/shard_map/ppermute | solution.py:74
  77.4 36.5 %collective-permute-start.3 = (bf16[32,8,768]{2,1,0:T(8,128)(2,1)S(1)}, bf16[32,8,768]{2,1,0:T(8,128)(2,1)S(1)}, u32[]{:S(2)}, u32[]{:S(2)}) collective-permute-start(bf16[32,8,768]{2,1,0:T(8,128)(2,1)S(1)} %get-tuple-element.63), channel_id=1, source_target_pairs={{0,3},{1,2},{2,1},{3,0},{4,7},{5,6},{6,5},{7,4},{8,11},{9,10},{10,... | collective-permute-start | bytes 1179656 | tf_op jit(solution)/shard_map/ppermute | solution.py:74
  120.0 4.4 %collective-permute-start.4 = (f32[2,64,8]{2,1,0:T(8,128)S(1)}, f32[2,64,8]{2,1,0:T(8,128)S(1)}, u32[]{:S(2)}, u32[]{:S(2)}) collective-permute-start(f32[2,64,8]{2,1,0:T(8,128)S(1)} %pad_maximum_fusion), channel_id=1, source_target_pairs={{0,3},{1,2},{2,1},{3,0},{4,7},{5,6},{6,5},{7,4},{8,11},{9,10},{10,... | collective-permute-start | bytes 12296 | tf_op jit(solution)/shard_map/ppermute | solution.py:115
  125.1 22.5 %all-to-all-start.2 = ((f32[2,64,8]{2,0,1:T(2,128)}), f32[2,64,8]{2,0,1:T(2,128)S(1)}, u32[]{:S(2)}, u32[]{:S(2)}) async-start(f32[2,64,8]{2,0,1:T(2,128)} %copy.46), calls=%async_computation.2 | async-start | bytes 131072 | tf_op jit(solution)/shard_map/all_to_all | solution.py:117
  137.6 10.8 %collective-permute-start.5 = (f32[4,512]{1,0:T(4,128)S(1)}, f32[4,512]{1,0:T(4,128)S(1)}, u32[]{:S(2)}, u32[]{:S(2)}) collective-permute-start(f32[4,512]{1,0:T(4,128)S(1)} %maximum_maximum_fusion.2), channel_id=1, source_target_pairs={{0,1},{1,0},{2,3},{3,2},{4,5},{5,4},{6,7},{7,6},{8,9},{9,8},{10,11... | collective-permute-start | bytes 24584 | tf_op jit(solution)/shard_map/ppermute | solution.py:112

commit v3 on v0

--- a/solution.py
+++ b/solution.py
@@ -1,6 +1,8 @@
 import jax
 import jax.numpy as jnp
 from jax import lax
+from jax.experimental import pallas as pl
+from jax.experimental.pallas import tpu as pltpu
 from jax.sharding import PartitionSpec as P
 
 
@@ -15,6 +17,20 @@
     return (values * lax.rsqrt(jnp.sum(values * values, axis=-1, keepdims=True) + EPS)).astype(
         jnp.bfloat16
     )
+
+
+def _stage_kernel(source_ref, staged_ref):
+    pltpu.sync_copy(source_ref, staged_ref)
+
+
+def stage_in_vmem(source):
+    return pl.pallas_call(
+        _stage_kernel,
+        out_shape=jax.ShapeDtypeStruct(source.shape, source.dtype),
+        in_specs=[pl.BlockSpec(memory_space=pl.ANY)],
+        out_specs=pl.BlockSpec(memory_space=pltpu.VMEM),
+        cost_estimate=pl.CostEstimate(flops=0, transcendentals=0, bytes_accessed=2 * source.nbytes),
+    )(source)
 
 
 def lent_scores(lent, row_valid, listed, columns, col_limit):
@@ -48,7 +64,7 @@
     own_counts = lax.dynamic_slice_in_dim(counts, first, owned)
     positions = jnp.arange(quarter, dtype=jnp.int32)
     col_sources = []
-    for lane, unit in ((my_lane, own_unit), (lane_p, other_unit)):
+    for lane, unit in ((my_lane, stage_in_vmem(own_unit)), (lane_p, stage_in_vmem(other_unit))):
         col_limit = (own_counts - lane * quarter).astype(jnp.int32)
         col_sources.append((unit, col_limit))
     slice_offsets = jnp.arange(slice_rows, dtype=jnp.int32)

time: 146 us -> 148 us (1.014)
  Pallas kernels: 0 us -> 7.14 us
  matrix products: 35 us -> 29.6 us
  waiting for transfers between devices: 48.7 us -> 46.8 us
  local copies, waits for them, and re-layouts: 11.5 us -> 13.2 us
    pallas_call x0 -> x2, Pallas kernels: none -> 7.14 us  [stage_in_vmem(): pl.pallas_call(_stage_kernel, out_shape=jax.ShapeDtypeStruct(source.shape...]
    dot_general x8, matrix products: 35 us -> 29.6 us  [lent_scores(): jnp.einsum('rd,kcd->rkc', flat_rows, columns, preferred_element_type=jnp....]
    all_to_all x2, waiting for transfers between devices: 32.6 us -> 29 us  [device_body(): lax.all_to_all(outbound, 'gx', split_axis=0, concat_axis=0, tiled=True)]
    unnamed x6 -> x14, local copies, waits for them, and re-layouts: 0.02 us -> 1.73 us
    ppermute x1, waiting for transfers between devices: 4.32 us -> 6.02 us  [device_body(): other_unit = lax.ppermute(own_unit, 'gy', pair_p)]
  transfers between devices with their start and end apart: 8 -> 8, of which waited for: 5 -> 5; matrix products, arithmetic and copies ran while one was open for 25% -> 22% of each run, Pallas kernels for 0% -> 5%
where the time goes in v3:
time: 148 us; the launch traced here: 147 us
  waiting for transfers between devices  46.8 us (32%)
  starting transfers between devices  40.6 us (27%)
  matrix products  29.6 us (20%)
  local copies, waits for them, and re-layouts  13.2 us (9%)
  other arithmetic  9.62 us (6%)
  Pallas kernels  7.14 us (5%)
    dot_general x8, matrix products, lent_scores(): jnp.einsum('rd,kcd->rkc', flat_rows, columns, preferred_element_type=jnp....  29.6 us
    all_to_all x2, waiting for transfers between devices, device_body(): lax.all_to_all(outbound, 'gx', split_axis=0, concat_axis=0, tiled=True)  29 us
    all_to_all x2, starting transfers between devices, device_body(): lax.all_to_all(outbound, 'gx', split_axis=0, concat_axis=0, tiled=True)  19.4 us
    all_to_all x1, starting transfers between devices, device_body(): lax.all_to_all(row_mine, 'gx', split_axis=1, concat_axis=1, tiled=True)  12.3 us
    all_to_all x1, waiting for transfers between devices, device_body(): lax.all_to_all(row_mine, 'gx', split_axis=1, concat_axis=1, tiled=True)  9.97 us
    pallas_call x2, Pallas kernels, stage_in_vmem(): pl.pallas_call(_stage_kernel, out_shape=jax.ShapeDtypeStruct(source.shape...  7.14 us
    gather x2, local copies, waits for them, and re-layouts, device_body(): outbound = own_pieces[outgoing_sent_block, outgoing_sent_piece]  7 us
    ppermute x1, waiting for transfers between devices, device_body(): other_unit = lax.ppermute(own_unit, 'gy', pair_p)  6.02 us
  transfers between devices with their start and end apart: 8, of which 5 were waited for; matrix products, arithmetic and copies ran while one was open for 22% of the time, Pallas kernels for 5%

profile of v3, /device:TPU:1, one launch (start us, length us, event | category | flops | bytes accessed | tf_op | source)
XLA Modules:
  0.0 147.4 jit_solution(8831563548492918485)
XLA Ops:
  0.9 2.6 %fusion = f32[4,512]{1,0:T(4,128)S(1)} fusion(bf16[4,512,768]{2,1,0:T(8,128)(2,1)} %param.4), kind=kLoop, calls=%fused_computation.6 | loop fusion | flops 4716544 | bytes 3153920 | tf_op jit(solution)/shard_map/reduce_sum | solution.py:17
  6.0 3.5 %gather_fusion.1 = bf16[64,8,768]{2,1,0:T(8,128)(2,1)} fusion(bf16[4,64,8,768]{3,2,1,0:T(8,128)(2,1)} %fusion.71, s32[64]{0:T(128)S(1)} %fusion.65), kind=kCustom, calls=%fused_computation.1 | custom fusion | bytes 1573376 | tf_op jit(solution)/shard_map/gather | solution.py:83
  9.5 13.3 %all-to-all-start = ((bf16[64,8,768]{2,1,0:T(8,128)(2,1)}), bf16[64,8,768]{2,1,0:T(8,128)(2,1)}, u32[]{:S(2)}, u32[]{:S(2)}) async-start(bf16[64,8,768]{2,1,0:T(8,128)(2,1)} %gather_fusion.1), calls=%async_computation | async-start | bytes 1572864 | tf_op jit(solution)/shard_map/all_to_all | solution.py:84
  22.9 2.3 %fusion.1.source_ref = bf16[4,512,768]{2,1,0:T(8,128)(2,1)} fusion(bf16[4,512,768]{2,1,0:T(8,128)(2,1)S(1)} %copy-done.1, f32[4,512]{1,0:T(4,128)S(1)} %add_rsqrt_fusion), kind=kLoop, calls=%fused_computation.7 | loop fusion | flops 4718592 | bytes 6299648 | tf_op jit(solution)/shard_map/convert_element_type | solution.py:17
  28.7 3.5 %gather_fusion.3 = bf16[64,8,768]{2,1,0:T(8,128)(2,1)} fusion(bf16[4,64,8,768]{3,2,1,0:T(8,128)(2,1)} %fusion.71, s32[64]{0:T(128)S(1)} %fusion.64), kind=kCustom, calls=%fused_computation.3 | custom fusion | bytes 1573376 | tf_op jit(solution)/shard_map/gather | solution.py:83
  32.6 13.2 %all-to-all-done = bf16[64,8,768]{2,1,0:T(8,128)(2,1)} async-done(((bf16[64,8,768]{2,1,0:T(8,128)(2,1)}), bf16[64,8,768]{2,1,0:T(8,128)(2,1)}, u32[]{:S(2)}, u32[]{:S(2)}) %all-to-all-start) | async-done | bytes 786464 | tf_op jit(solution)/shard_map/all_to_all | solution.py:84
  45.8 6.1 %all-to-all-start.1 = ((bf16[64,8,768]{2,1,0:T(8,128)(2,1)}), bf16[64,8,768]{2,1,0:T(8,128)(2,1)}, u32[]{:S(2)}, u32[]{:S(2)}) async-start(bf16[64,8,768]{2,1,0:T(8,128)(2,1)} %gather_fusion.3), calls=%async_computation.1 | async-start | bytes 1572864 | tf_op jit(solution)/shard_map/all_to_all | solution.py:84
  52.5 2.6 %collective-permute-start = (bf16[64,8,768]{2,1,0:T(8,128)(2,1)}, bf16[64,8,768]{2,1,0:T(8,128)(2,1)}, u32[]{:S(2)}, u32[]{:S(2)}) collective-permute-start(bf16[64,8,768]{2,1,0:T(8,128)(2,1)} %all-to-all-done), channel_id=1, source_target_pairs={{0,3},{1,2},{2,1},{3,0},{4,7},{5,6},{6,5},{7,4},{8,11},{9,10},{10,... | collective-permute-start | bytes 2359304 | tf_op jit(solution)/shard_map/ppermute | solution.py:85
  55.0 3.6 %shard_map.46 = bf16[4,512,768]{2,1,0:T(8,128)(2,1)} custom-call(bf16[4,512,768]{2,1,0:T(8,128)(2,1)} %fusion.1.source_ref), custom_call_target="tpu_custom_call" | custom-call | bytes 6291456 | tf_op jit(solution)/shard_map/pallas_call | solution.py:27
  59.1 15.8 %all-to-all-done.1 = bf16[64,8,768]{2,1,0:T(8,128)(2,1)} async-done(((bf16[64,8,768]{2,1,0:T(8,128)(2,1)}), bf16[64,8,768]{2,1,0:T(8,128)(2,1)}, u32[]{:S(2)}, u32[]{:S(2)}) %all-to-all-start.1) | async-done | bytes 786464 | tf_op jit(solution)/shard_map/all_to_all | solution.py:84
  74.8 2.5 %collective-permute-start.2 = (bf16[64,8,768]{2,1,0:T(8,128)(2,1)}, bf16[64,8,768]{2,1,0:T(8,128)(2,1)}, u32[]{:S(2)}, u32[]{:S(2)}) collective-permute-start(bf16[64,8,768]{2,1,0:T(8,128)(2,1)} %all-to-all-done.1), channel_id=1, source_target_pairs={{0,3},{1,2},{2,1},{3,0},{4,7},{5,6},{6,5},{7,4},{8,11},{9,10},{10,... | collective-permute-start | bytes 2359304 | tf_op jit(solution)/shard_map/ppermute | solution.py:85
  77.3 4.3 %fusion.2 = (f32[4,512]{1,0:T(4,128)S(1)}, f32[64,8]{1,0:T(8,128)S(1)}) fusion(pred[4,512]{1,0:T(4,128)(4,1)S(1)} %iota_compare_fusion.5, pred[64,8,4]{1,2,0:T(4,128)(4,1)S(1)} %get-tuple-element.60, bf16[4,512,768]{2,1,0:T(8,128)(2,1)} %shard_map.46, bf16[64,8,768]{2,1,0:T(8,128)(2,1)} %all-to-all-done), kind=kOutput, calls=%fused_computation.16 | convolution fusion | flops 1614804480 | bytes 3946496 | tf_op jit(solution)/shard_map/rd,kcd->rkc/dot_general | solution.py:40
  81.6 3.5 %fusion.8 = (f32[4,512]{1,0:T(4,128)S(1)}, f32[64,8]{1,0:T(8,128)S(1)}) fusion(pred[64,8,4]{1,2,0:T(4,128)(4,1)S(1)} %get-tuple-element.59, pred[4,512]{1,0:T(4,128)(4,1)S(1)} %iota_compare_fusion.5, bf16[4,512,768]{2,1,0:T(8,128)(2,1)S(1)} %copy-done.3, bf16[64,8,768]{2,1,0:T(8,128)(2,1)} %collective-permute-done), kind=kOutput, calls=%fused_computation.22 | convolution fusion | flops 1614804480 | bytes 3946496 | tf_op jit(solution)/shard_map/rd,kcd->rkc/dot_general | solution.py:40
  85.1 3.5 %fusion.6 = (f32[4,512]{1,0:T(4,128)S(1)}, f32[64,8]{1,0:T(8,128)S(1)}) fusion(pred[64,8,4]{1,2,0:T(4,128)(4,1)S(1)} %get-tuple-element.58, pred[4,512]{1,0:T(4,128)(4,1)S(1)} %iota_compare_fusion.5, bf16[4,512,768]{2,1,0:T(8,128)(2,1)S(1)} %copy-done.3, bf16[64,8,768]{2,1,0:T(8,128)(2,1)} %all-to-all-done.1), kind=kOutput, calls=%fused_computation.20 | convolution fusion | flops 1614804480 | bytes 3946496 | tf_op jit(solution)/shard_map/rd,kcd->rkc/dot_general | solution.py:40
  88.6 6.0 %collective-permute-done.1.source_ref = bf16[4,512,768]{2,1,0:T(8,128)(2,1)S(1)} collective-permute-done((bf16[4,512,768]{2,1,0:T(8,128)(2,1)}, bf16[4,512,768]{2,1,0:T(8,128)(2,1)S(1)}, u32[]{:S(2)}, u32[]{:S(2)}) %collective-permute-start.1) | collective-permute-done | bytes 3145760 | tf_op jit(solution)/shard_map/ppermute | solution.py:62
  96.3 3.6 %shard_map.47 = bf16[4,512,768]{2,1,0:T(8,128)(2,1)} custom-call(bf16[4,512,768]{2,1,0:T(8,128)(2,1)} %copy-done.2), custom_call_target="tpu_custom_call" | custom-call | bytes 6291456 | tf_op jit(solution)/shard_map/pallas_call | solution.py:27
  99.9 4.3 %fusion.4 = (f32[4,512]{1,0:T(4,128)S(1)}, f32[64,8]{1,0:T(8,128)S(1)}) fusion(pred[4,512]{1,0:T(4,128)(4,1)S(1)} %iota_compare_fusion.4, pred[64,8,4]{1,2,0:T(4,128)(4,1)S(1)} %get-tuple-element.60, bf16[4,512,768]{2,1,0:T(8,128)(2,1)} %shard_map.47, bf16[64,8,768]{2,1,0:T(8,128)(2,1)} %all-to-all-done), kind=kOutput, calls=%fused_computation.18 | convolution fusion | flops 1614804480 | bytes 3946496 | tf_op jit(solution)/shard_map/rd,kcd->rkc/dot_general | solution.py:40
  104.2 3.5 %fusion.12 = (f32[4,512]{1,0:T(4,128)S(1)}, f32[64,8]{1,0:T(8,128)S(1)}) fusion(pred[64,8,4]{1,2,0:T(4,128)(4,1)S(1)} %get-tuple-element.59, pred[4,512]{1,0:T(4,128)(4,1)S(1)} %iota_compare_fusion.4, bf16[4,512,768]{2,1,0:T(8,128)(2,1)S(1)} %copy-done.5, bf16[64,8,768]{2,1,0:T(8,128)(2,1)} %collective-permute-done), kind=kOutput, calls=%fused_computation.26 | convolution fusion | flops 1614804480 | bytes 3946496 | tf_op jit(solution)/shard_map/rd,kcd->rkc/dot_general | solution.py:40
  107.7 3.6 %fusion.10 = (f32[4,512]{1,0:T(4,128)S(1)}, f32[64,8]{1,0:T(8,128)S(1)}) fusion(pred[64,8,4]{1,2,0:T(4,128)(4,1)S(1)} %get-tuple-element.58, pred[4,512]{1,0:T(4,128)(4,1)S(1)} %iota_compare_fusion.4, bf16[4,512,768]{2,1,0:T(8,128)(2,1)S(1)} %copy-done.5, bf16[64,8,768]{2,1,0:T(8,128)(2,1)} %all-to-all-done.1), kind=kOutput, calls=%fused_computation.24 | convolution fusion | flops 1614804480 | bytes 3946496 | tf_op jit(solution)/shard_map/rd,kcd->rkc/dot_general | solution.py:40
  111.4 3.5 %fusion.14 = (f32[4,512]{1,0:T(4,128)S(1)}, f32[64,8]{1,0:T(8,128)S(1)}) fusion(pred[64,8,4]{1,2,0:T(4,128)(4,1)S(1)} %get-tuple-element.57, pred[4,512]{1,0:T(4,128)(4,1)S(1)} %iota_compare_fusion.5, bf16[4,512,768]{2,1,0:T(8,128)(2,1)S(1)} %copy-done.4, bf16[64,8,768]{2,1,0:T(8,128)(2,1)} %collective-permute-done.2), kind=kOutput, calls=%fused_computation.28 | convolution fusion | flops 1614804480 | bytes 3946496 | tf_op jit(solution)/shard_map/rd,kcd->rkc/dot_general | solution.py:40
  114.9 3.5 %fusion.16 = (f32[4,512]{1,0:T(4,128)S(1)}, f32[64,8]{1,0:T(8,128)S(1)}) fusion(pred[64,8,4]{1,2,0:T(4,128)(4,1)S(1)} %get-tuple-element.57, pred[4,512]{1,0:T(4,128)(4,1)S(1)} %iota_compare_fusion.4, bf16[4,512,768]{2,1,0:T(8,128)(2,1)S(1)} %copy-done.5, bf16[64,8,768]{2,1,0:T(8,128)(2,1)} %collective-permute-done.2), kind=kOutput, calls=%fused_computation.30 | convolution fusion | flops 1614804480 | bytes 3946496 | tf_op jit(solution)/shard_map/rd,kcd->rkc/dot_general | solution.py:40
  118.4 2.6 %collective-permute-start.3 = (f32[2,64,8]{2,1,0:T(8,128)S(1)}, f32[2,64,8]{2,1,0:T(8,128)S(1)}, u32[]{:S(2)}, u32[]{:S(2)}) collective-permute-start(f32[2,64,8]{2,1,0:T(8,128)S(1)} %pad_maximum_fusion), channel_id=1, source_target_pairs={{0,3},{1,2},{2,1},{3,0},{4,7},{5,6},{6,5},{7,4},{8,11},{9,10},{10,... | collective-permute-start | bytes 12296 | tf_op jit(solution)/shard_map/ppermute | solution.py:115
  123.5 12.3 %all-to-all-start.2 = ((f32[2,64,8]{2,0,1:T(2,128)}), f32[2,64,8]{2,0,1:T(2,128)S(1)}, u32[]{:S(2)}, u32[]{:S(2)}) async-start(f32[2,64,8]{2,0,1:T(2,128)} %copy.31), calls=%async_computation.2 | async-start | bytes 131072 | tf_op jit(solution)/shard_map/all_to_all | solution.py:117
  136.0 10.0 %all-to-all-done.2 = f32[2,64,8]{2,0,1:T(2,128)S(1)} async-done(((f32[2,64,8]{2,0,1:T(2,128)}), f32[2,64,8]{2,0,1:T(2,128)S(1)}, u32[]{:S(2)}, u32[]{:S(2)}) %all-to-all-start.2) | async-done | bytes 4128 | tf_op jit(solution)/shard_map/all_to_all | solution.py:117
  (75 shorter events, 14.1 us)
Async XLA Ops:
  0.0 3.6 %copy-start.1 = (bf16[4,512,768]{2,1,0:T(8,128)(2,1)S(1)}, bf16[4,512,768]{2,1,0:T(8,128)(2,1)}, u32[]{:S(2)}) copy-start(bf16[4,512,768]{2,1,0:T(8,128)(2,1)} %param.4) | copy-start | bytes 9437188
  9.5 36.3 %all-to-all-start = ((bf16[64,8,768]{2,1,0:T(8,128)(2,1)}), bf16[64,8,768]{2,1,0:T(8,128)(2,1)}, u32[]{:S(2)}, u32[]{:S(2)}) async-start(bf16[64,8,768]{2,1,0:T(8,128)(2,1)} %gather_fusion.1), calls=%async_computation | async-start | bytes 1572864 | tf_op jit(solution)/shard_map/all_to_all | solution.py:84
  22.9 3.8 %copy-start = (s32[256]{0:T(256)S(1)}, s32[256]{0:T(256)}, u32[]{:S(2)}) copy-start(s32[256]{0:T(256)} %param.7) | copy-start | bytes 3076
  22.9 5.6 %copy-start.6 = (s32[2,64,64,2]{2,3,1,0:T(2,128)S(1)}, s32[2,64,64,2]{2,3,1,0:T(2,128)}, u32[]{:S(2)}) copy-start(s32[2,64,64,2]{2,3,1,0:T(2,128)} %param.6) | copy-start | bytes 196612
  25.2 69.5 %collective-permute-start.1 = (bf16[4,512,768]{2,1,0:T(8,128)(2,1)}, bf16[4,512,768]{2,1,0:T(8,128)(2,1)S(1)}, u32[]{:S(2)}, u32[]{:S(2)}) collective-permute-start(bf16[4,512,768]{2,1,0:T(8,128)(2,1)} %fusion.1.source_ref), channel_id=1, source_target_pairs={{0,1},{1,0},{2,3},{3,2},{4,5},{5,4},{6,7},{7,6},{8,9},{9,8},{10,11... | collective-permute-start | bytes 9437192 | tf_op jit(solution)/shard_map/ppermute | solution.py:62
  45.8 29.0 %all-to-all-start.1 = ((bf16[64,8,768]{2,1,0:T(8,128)(2,1)}), bf16[64,8,768]{2,1,0:T(8,128)(2,1)}, u32[]{:S(2)}, u32[]{:S(2)}) async-start(bf16[64,8,768]{2,1,0:T(8,128)(2,1)} %gather_fusion.3), calls=%async_computation.1 | async-start | bytes 1572864 | tf_op jit(solution)/shard_map/all_to_all | solution.py:84
  52.5 29.1 %collective-permute-start = (bf16[64,8,768]{2,1,0:T(8,128)(2,1)}, bf16[64,8,768]{2,1,0:T(8,128)(2,1)}, u32[]{:S(2)}, u32[]{:S(2)}) collective-permute-start(bf16[64,8,768]{2,1,0:T(8,128)(2,1)} %all-to-all-done), channel_id=1, source_target_pairs={{0,3},{1,2},{2,1},{3,0},{4,7},{5,6},{6,5},{7,4},{8,11},{9,10},{10,... | collective-permute-start | bytes 2359304 | tf_op jit(solution)/shard_map/ppermute | solution.py:85
  74.8 36.6 %collective-permute-start.2 = (bf16[64,8,768]{2,1,0:T(8,128)(2,1)}, bf16[64,8,768]{2,1,0:T(8,128)(2,1)}, u32[]{:S(2)}, u32[]{:S(2)}) collective-permute-start(bf16[64,8,768]{2,1,0:T(8,128)(2,1)} %all-to-all-done.1), channel_id=1, source_target_pairs={{0,3},{1,2},{2,1},{3,0},{4,7},{5,6},{6,5},{7,4},{8,11},{9,10},{10,... | collective-permute-start | bytes 2359304 | tf_op jit(solution)/shard_map/ppermute | solution.py:85
  77.3 4.3 %copy-start.3 = (bf16[4,512,768]{2,1,0:T(8,128)(2,1)S(1)}, bf16[4,512,768]{2,1,0:T(8,128)(2,1)}, u32[]{:S(2)}) copy-start(bf16[4,512,768]{2,1,0:T(8,128)(2,1)} %shard_map.46) | copy-start | bytes 9437188
  94.6 1.7 %copy-start.2 = (bf16[4,512,768]{2,1,0:T(8,128)(2,1)}, bf16[4,512,768]{2,1,0:T(8,128)(2,1)S(1)}, u32[]{:S(2)}) copy-start(bf16[4,512,768]{2,1,0:T(8,128)(2,1)S(1)} %collective-permute-done.1.source_ref) | copy-start | bytes 9437188
  99.9 4.3 %copy-start.5 = (bf16[4,512,768]{2,1,0:T(8,128)(2,1)S(1)}, bf16[4,512,768]{2,1,0:T(8,128)(2,1)}, u32[]{:S(2)}) copy-start(bf16[4,512,768]{2,1,0:T(8,128)(2,1)} %shard_map.47) | copy-start | bytes 9437188
  107.7 3.7 %copy-start.4 = (bf16[4,512,768]{2,1,0:T(8,128)(2,1)S(1)}, bf16[4,512,768]{2,1,0:T(8,128)(2,1)}, u32[]{:S(2)}) copy-start(bf16[4,512,768]{2,1,0:T(8,128)(2,1)} %shard_map.46) | copy-start | bytes 9437188
  118.4 4.4 %collective-permute-start.3 = (f32[2,64,8]{2,1,0:T(8,128)S(1)}, f32[2,64,8]{2,1,0:T(8,128)S(1)}, u32[]{:S(2)}, u32[]{:S(2)}) collective-permute-start(f32[2,64,8]{2,1,0:T(8,128)S(1)} %pad_maximum_fusion), channel_id=1, source_target_pairs={{0,3},{1,2},{2,1},{3,0},{4,7},{5,6},{6,5},{7,4},{8,11},{9,10},{10,... | collective-permute-start | bytes 12296 | tf_op jit(solution)/shard_map/ppermute | solution.py:115
  123.5 22.4 %all-to-all-start.2 = ((f32[2,64,8]{2,0,1:T(2,128)}), f32[2,64,8]{2,0,1:T(2,128)S(1)}, u32[]{:S(2)}, u32[]{:S(2)}) async-start(f32[2,64,8]{2,0,1:T(2,128)} %copy.31), calls=%async_computation.2 | async-start | bytes 131072 | tf_op jit(solution)/shard_map/all_to_all | solution.py:117
  135.9 10.8 %collective-permute-start.4 = (f32[4,512]{1,0:T(4,128)S(1)}, f32[4,512]{1,0:T(4,128)S(1)}, u32[]{:S(2)}, u32[]{:S(2)}) collective-permute-start(f32[4,512]{1,0:T(4,128)S(1)} %maximum_maximum_fusion.2), channel_id=1, source_target_pairs={{0,1},{1,0},{2,3},{3,2},{4,5},{5,4},{6,7},{7,6},{8,9},{9,8},{10,11... | collective-permute-start | bytes 24584 | tf_op jit(solution)/shard_map/ppermute | solution.py:112
